TPU v7x, 128 devices: a whole 4x4x4 slice. The times are simulated.
128 devices in a mesh: dp: 8 (over x_lo, z), mp: 16 (over y, x_hi, core).
Axes of the slice: x: 4 (x_hi: 2, x_lo: 2; x = x_hi * 2 + x_lo), y: 4, z: 4, core: 2. Of those that a mesh axis runs over, the one named last changes fastest.
Arguments:
- tokens_in: bfloat16 [8192, 3072], P(('dp', 'mp')), may hold values from -6 to 6
- out_grad: bfloat16 [8192, 3072], P(('dp', 'mp')), may hold values from -0.29882812 to 0.29882812
- w_up: bfloat16 [12288, 3072], P('mp'), may hold values from -0.109375 to 0.109375
- w_down: bfloat16 [12288, 3072], P('mp'), may hold values from -0.0546875 to 0.0546875
- mask_up: int32 [96, 24], P('mp'), may hold values 0 or 1
- mask_down: int32 [96, 24], P('mp'), may hold values 0 or 1
- order_up: int32 [24], replicated, may hold values from 0 to 23, each once
- order_down: int32 [24], replicated, may hold values from 0 to 23, each once
- moment_one: float32 [2, 16, 24, 32, 3072], P(None, 'mp', 'dp'), may hold values from -1.8 to 1.8
- moment_two: float32 [2, 16, 24, 32, 3072], P(None, 'mp', 'dp'), may hold values from 0.03 to 1
Outputs:
- input_grad: bfloat16 [8192, 3072], P(('dp', 'mp'))
- update_step: bfloat16 [2, 12288, 3072], P(None, 'mp')
Inputs may be any that keep to these rules, and one draw needn't show every extreme that they name: `order_up`: each value of 0 to 23 appears once. `order_down`: each value of 0 to 23 appears once.
All inputs are finite; a program needn't handle non-finite values. No bound on the sum of `mask_up` or of `mask_down` on one device may be relied on, other than what follows from the above.
Results may differ from a plain program's by a relative error of at most 0.014.
Values may be sent and summed in bfloat16 or wider, within the bound.
No kernel may reach another device: no remote copies, remote signals or barrier semaphores. Data moves between devices by JAX's collectives and lax.ppermute only.
A program may use at most 128 MiB of HBM per device.

v0:
```python
import jax
import jax.numpy as jnp
from jax import lax
from jax.sharding import PartitionSpec as P

bias_first = 1.0 - 0.9**10
bias_second = 1.0 - 0.95**10


def expand_mask(blocks):
    block_rows, block_cols = blocks.shape
    wide = jnp.broadcast_to(
        blocks.astype(jnp.bfloat16)[:, None, :, None], (block_rows, 128, block_cols, 128)
    )
    return wide.reshape(block_rows * 128, block_cols * 128)


def adam_step(summed, moment_a, moment_b, weight_rows, mask_rows):
    first_new = 0.9 * moment_a + 0.1 * summed
    second_new = 0.95 * moment_b + 0.05 * summed * summed
    update = first_new / bias_first / (jnp.sqrt(second_new / bias_second) + 1e-08)
    return (mask_rows * (update + 0.1 * weight_rows)).astype(jnp.bfloat16)


def slot_places(order_table, owners, owned):
    return order_table % owners * owned + order_table // owners


def shards(
    tokens_in,
    out_grad,
    w_up,
    w_down,
    mask_up,
    mask_down,
    order_up,
    order_down,
    moment_one,
    moment_two,
):
    owners = lax.axis_size("dp")
    hidden_local, width = w_up.shape
    buckets = order_up.shape[0]
    owned = buckets // owners
    bucket_rows = hidden_local // buckets
    keep_up = expand_mask(mask_up)
    keep_down = expand_mask(mask_down)
    up_live = w_up * keep_up
    down_live = w_down * keep_down
    place_up = slot_places(order_up, owners, owned)
    place_down = slot_places(order_down, owners, owned)
    sorter_up = jnp.argsort(place_up)
    sorter_down = jnp.argsort(place_down)

    def owner_order(matrix, sorter):
        return matrix.reshape(buckets, bucket_rows, width)[sorter]

    feat_rows, grad_rows = (
        lax.all_gather(tokens_in, "mp", axis=0, tiled=True),
        lax.all_gather(out_grad, "mp", axis=0, tiled=True),
    )
    hidden_pre = jnp.einsum("td,fd->tf", feat_rows, up_live, preferred_element_type=jnp.float32)
    activation, gelu_back = jax.vjp(jax.nn.gelu, hidden_pre)
    act_low = activation.astype(jnp.bfloat16)
    grad_down = (
        jnp.einsum("tf,td->fd", act_low, grad_rows, preferred_element_type=jnp.float32) * keep_down
    ).astype(jnp.bfloat16)
    down_sorted = owner_order(grad_down, sorter_down)
    act_grad = jnp.einsum("td,fd->tf", grad_rows, down_live, preferred_element_type=jnp.float32)
    hidden_grad = gelu_back(act_grad)[0].astype(jnp.bfloat16)
    grad_up = (
        jnp.einsum("tf,td->fd", hidden_grad, feat_rows, preferred_element_type=jnp.float32)
        * keep_up
    ).astype(jnp.bfloat16)
    up_sorted = owner_order(grad_up, sorter_up)
    up_summed, down_summed = (
        lax.psum_scatter(up_sorted, "dp", scatter_dimension=0, tiled=True).astype(jnp.float32),
        lax.psum_scatter(down_sorted, "dp", scatter_dimension=0, tiled=True).astype(jnp.float32),
    )
    partial_term = jnp.dot(hidden_grad, up_live, preferred_element_type=jnp.float32)
    input_grad = lax.psum_scatter(
        lax.optimization_barrier(partial_term.astype(jnp.bfloat16))
        .astype(jnp.float32)
        .astype(jnp.bfloat16),
        "mp",
        scatter_dimension=0,
        tiled=True,
    )
    owner_index = lax.axis_index("dp")

    def owned_rows(matrix, sorter):
        chosen = lax.dynamic_slice_in_dim(sorter, owner_index * owned, owned, 0)
        return matrix.reshape(buckets, bucket_rows, width)[chosen].astype(jnp.float32)

    step_up = adam_step(
        up_summed,
        moment_one[0, 0],
        moment_two[0, 0],
        owned_rows(w_up, sorter_up),
        owned_rows(keep_up, sorter_up),
    )
    step_down = adam_step(
        down_summed,
        moment_one[1, 0],
        moment_two[1, 0],
        owned_rows(w_down, sorter_down),
        owned_rows(keep_down, sorter_down),
    )
    stacked = jnp.stack([step_up, step_down])
    all_steps = lax.all_gather(stacked, "dp", axis=1, tiled=True)
    update_up = all_steps[0][place_up].reshape(hidden_local, width)
    update_down = all_steps[1][place_down].reshape(hidden_local, width)
    return (input_grad, jnp.stack([update_up, update_down]))


def solution(mesh):
    placed = (
        P(("dp", "mp"), None),
        P(("dp", "mp"), None),
        P("mp", None),
        P("mp", None),
        P("mp", None),
        P("mp", None),
        P(),
        P(),
        P(None, "mp", "dp", None, None),
        P(None, "mp", "dp", None, None),
    )
    return jax.shard_map(
        shards,
        mesh=mesh,
        in_specs=placed,
        out_specs=(P(("dp", "mp"), None), P(None, "mp", None)),
        check_vma=False,
    )
```

profile of v0, /device:TPU:0, one launch (start us, length us, event | category | flops | bytes accessed | tf_op | source)
XLA Modules:
  0.0 491.1 jit_solution(12678287739695662379)
XLA Ops:
  7.2 0.0 all-gather.6.cloned.1.call-start
  7.2 0.7 all-gather.6.cloned.1.call-update
  7.9 0.0 all-gather.4.cloned.1.call-start
  7.9 0.7 all-gather.4.cloned.1.call-update
  8.6 0.0 reduce-scatter.6.cloned.1.call-start
  8.7 0.7 convert_element_type.54
  9.4 0.7 convert_element_type.53
  10.1 0.7 compare_select_fusion.1
  10.8 1.6 sort.31
  12.4 64.2 %all-gather.6.cloned.1.call-done = bf16[1024,3072]{1,0:T(8,128)(2,1)} async-done(((bf16[64,3072]{1,0:T(8,128)(2,1)}), bf16[1024,3072]{1,0:T(8,128)(2,1)}) %all-gather.6.cloned.1.call-update) | async-done | bytes 6291472 | tf_op jit(solution)/shard_map/all_gather | solution.py:59
  76.5 0.0 copy-start.2
  76.5 0.7 broadcast_in_dim.45
  77.2 0.0 copy-start
  77.2 2.4 copy-done
  79.6 1.0 copy-done.2
  80.6 8.4 %fusion.18 = f32[768,1024]{1,0:T(8,128)} fusion(bf16[1024,3072]{1,0:T(8,128)(2,1)} %all-gather.6.cloned.1.call-done, bf16[768,3072]{1,0:T(8,128)(2,1)S(1)} %copy-done.2, bf16[96,8,24,128]{3,2,1,0:T(8,128)(2,1)S(1)} %bitcast.98), kind=kOutput, calls=%fused_computation.42 | convolution fusion | flops 4834197504 | bytes 18874368 | tf_op jit(solution)/shard_map/td,fd->tf/dot_general | solution.py:62
  89.0 51.5 %all-gather.4.cloned.1.call-done = bf16[1024,3072]{1,0:T(8,128)(2,1)} async-done(((bf16[64,3072]{1,0:T(8,128)(2,1)}), bf16[1024,3072]{1,0:T(8,128)(2,1)}) %all-gather.4.cloned.1.call-update) | async-done | bytes 6291472 | tf_op jit(solution)/shard_map/all_gather | solution.py:60
  140.4 0.0 slice-start
  140.4 0.0 slice-start.2
  140.4 0.7 broadcast_in_dim.44
  141.1 0.0 copy-start.1
  141.1 0.0 slice-start.1
  141.1 0.0 slice-start.3
  141.1 13.8 %fusion.8 = bf16[1024,768]{0,1:T(8,128)(2,1)} fusion(f32[768,1024]{1,0:T(8,128)} %fusion.18, bf16[1024,3072]{1,0:T(8,128)(2,1)} %all-gather.4.cloned.1.call-done, bf16[768,3072]{1,0:T(8,128)(2,1)} %param.13, bf16[96,8,24,128]{3,2,1,0:T(8,128)(2,1)S(1)} %bitcast.103), kind=kOutput, calls=%fused_computation.26 | convolution fusion | flops 4849926144 | bytes 20447232 | tf_op jit(solution)/shard_map/td,fd->tf/dot_general | solution.py:69
  155.0 0.0 copy-done.1
  155.0 0.0 slice-done
  155.0 0.0 slice-done.2
  155.0 0.0 slice-done.1
  155.0 0.0 slice-done.3
  155.0 8.5 %multiply_convert_fusion.1 = bf16[768,3072]{1,0:T(8,128)(2,1)} fusion(bf16[1024,768]{0,1:T(8,128)(2,1)} %fusion.8, bf16[1024,3072]{1,0:T(8,128)(2,1)S(1)} %bitcast.114, bf16[96,8,24,128]{3,2,1,0:T(8,128)(2,1)S(1)} %bitcast.102), kind=kOutput, calls=%fused_computation.10 | convolution fusion | flops 4838916096 | bytes 17301504 | tf_op jit(solution)/shard_map/tf,td->fd/dot_general | solution.py:72
  163.5 5.6 %gather_fusion.1 = bf16[24,32,3072]{2,1,0:T(8,128)(2,1)} fusion(bf16[24,32,3072]{2,1,0:T(8,128)(2,1)} %bitcast.106, s32[1024]{0:T(1024)S(1)} %pad_clamp_fusion.4), kind=kCustom, calls=%fused_computation.1 | custom fusion | bytes 9437280 | tf_op jit(solution)/shard_map/gather | solution.py:56
  169.1 0.0 copy-start.3
  169.1 0.0 reduce-scatter.6.cloned.1.call-update
  169.1 0.2 reduce-scatter.8.cloned.1.call-start
  169.3 0.4 copy-done.3
  169.8 1.6 sort.32
  171.4 11.1 %multiply_convert_fusion = bf16[768,3072]{1,0:T(8,128)(2,1)} fusion(bf16[1024,3072]{1,0:T(8,128)(2,1)} %all-gather.4.cloned.1.call-done, bf16[96,8,24,128]{3,2,1,0:T(8,128)(2,1)} %bitcast.104, f32[768,1024]{1,0:T(8,128)} %fusion.18), kind=kOutput, calls=%fused_computation.9 | convolution fusion | flops 4845993984 | bytes 18874368 | tf_op jit(solution)/shard_map/tf,td->fd/dot_general | solution.py:66
  182.5 5.5 %gather_fusion.4 = bf16[24,32,3072]{2,1,0:T(8,128)(2,1)} fusion(bf16[24,32,3072]{2,1,0:T(8,128)(2,1)} %bitcast.105, s32[1024]{0:T(1024)S(1)} %pad_clamp_fusion.2), kind=kCustom, calls=%fused_computation.4 | custom fusion | bytes 9437280 | tf_op jit(solution)/shard_map/gather | solution.py:56
  188.0 0.0 reduce-scatter.8.cloned.1.call-update
  188.0 0.0 all-gather.8.cloned.1.call-start
  188.1 0.1 broadcast_in_dim.46
  188.2 0.1 broadcast_in_dim.51
  188.3 0.1 compare_select_fusion.3
  188.4 2.8 broadcast_in_dim.48
  191.2 3.0 gather_fusion
  194.2 3.0 gather_fusion.2
  197.2 2.8 broadcast_in_dim.53
  200.0 3.0 gather_fusion.3
  202.9 3.0 gather_fusion.5
  205.9 19.5 %reduce-scatter.6.cloned.1.call-done = bf16[3,32,3072]{2,1,0:T(8,128)(2,1)} async-done(((bf16[24,32,3072]{2,1,0:T(8,128)(2,1)}), bf16[3,32,3072]{2,1,0:T(8,128)(2,1)}) %reduce-scatter.6.cloned.1.call-update) | async-done | bytes 589840 | tf_op jit(solution)/shard_map/reduce_scatter | solution.py:77
  225.4 59.2 %reduce-scatter.8.cloned.1.call-done = bf16[3,32,3072]{2,1,0:T(8,128)(2,1)} async-done(((bf16[24,32,3072]{2,1,0:T(8,128)(2,1)}), bf16[3,32,3072]{2,1,0:T(8,128)(2,1)}) %reduce-scatter.8.cloned.1.call-update) | async-done | bytes 589840 | tf_op jit(solution)/shard_map/reduce_scatter | solution.py:78
  284.6 4.7 fusion.39
  289.3 1.1 pad_maximum_fusion.1
  290.4 0.0 all-gather.8.cloned.1.call-update
  290.4 0.0 reduce-scatter.4.cloned.1.call-start
  290.5 0.6 copy-done.4
  291.1 10.8 %convolution_convert_fusion = bf16[1024,3072]{1,0:T(8,128)(2,1)} fusion(bf16[1024,768]{0,1:T(8,128)(2,1)S(1)} %copy-done.4, bf16[768,3072]{1,0:T(8,128)(2,1)} %param.12, bf16[96,8,24,128]{3,2,1,0:T(8,128)(2,1)} %bitcast.99), kind=kOutput, calls=%fused_computation.11 | convolution fusion | flops 4837343232 | bytes 17301504 | tf_op jit(solution)/shard_map/dot_general | solution.py:80
  301.9 0.0 reduce-scatter.4.cloned.1.call-update
  302.0 89.2 %all-gather.8.cloned.1.call-done = bf16[2,24,32,3072]{3,2,1,0:T(8,128)(2,1)} async-done(((bf16[2,3,32,3072]{3,2,1,0:T(8,128)(2,1)}), bf16[2,24,32,3072]{3,2,1,0:T(8,128)(2,1)}) %all-gather.8.cloned.1.call-update) | async-done | bytes 9437200 | tf_op jit(solution)/shard_map/all_gather | solution.py:110
  391.2 9.0 %slice_bitcast_fusion.1 = (bf16[24,32,3072]{2,1,0:T(8,128)(2,1)}, bf16[24,32,3072]{2,1,0:T(8,128)(2,1)}) fusion(bf16[2,24,32,3072]{3,2,1,0:T(8,128)(2,1)} %all-gather.8.cloned.1.call-done), kind=kLoop, calls=%fused_computation.16 | loop fusion | bytes 18874368 | tf_op jit(solution)/shard_map/squeeze | solution.py:111
  400.1 5.5 %gather_fusion.6 = bf16[24,32,3072]{2,1,0:T(8,128)(2,1)} fusion(bf16[24,32,3072]{2,1,0:T(8,128)(2,1)} %get-tuple-element.10, s32[1024]{0:T(1024)S(1)} %pad_clamp_fusion.1), kind=kCustom, calls=%fused_computation.6 | custom fusion | bytes 9437280 | tf_op jit(solution)/shard_map/gather | solution.py:111
  405.7 5.8 %gather_fusion.7 = bf16[24,32,3072]{2,1,0:T(8,128)(2,1)} fusion(bf16[24,32,3072]{2,1,0:T(8,128)(2,1)} %get-tuple-element.11, s32[1024]{0:T(1024)S(1)} %pad_clamp_fusion), kind=kCustom, calls=%fused_computation.7 | custom fusion | bytes 9437280 | tf_op jit(solution)/shard_map/gather | solution.py:112
  411.5 9.1 %pad_maximum_fusion = bf16[2,768,3072]{2,1,0:T(8,128)(2,1)} fusion(bf16[1,768,3072]{2,1,0:T(8,128)(2,1)} %bitcast.97, bf16[1,768,3072]{2,1,0:T(8,128)(2,1)} %bitcast.96), kind=kLoop, calls=%fused_computation.8 | loop fusion | flops 4718592 | bytes 18874368 | tf_op jit(solution)/shard_map/stack | solution.py:113
  420.5 63.7 %reduce-scatter.4.cloned.1.call-done = bf16[64,3072]{1,0:T(8,128)(2,1)} async-done(((bf16[1024,3072]{1,0:T(8,128)(2,1)}), bf16[64,3072]{1,0:T(8,128)(2,1)}) %reduce-scatter.4.cloned.1.call-update) | async-done | bytes 393232 | tf_op jit(solution)/shard_map/reduce_scatter | solution.py:81
  (16 shorter events, 0.1 us)
Async XLA Ops:
  7.2 69.4 %all-gather.6.cloned.1.call-start = ((), (), s32[]{:S(2)}) async-start(), calls=%async_computation.4 | async-start | bytes 6684672 | tf_op jit(solution)/shard_map/all_gather | solution.py:59
  7.9 132.5 %all-gather.4.cloned.1.call-start = ((), (), s32[]{:S(2)}) async-start(), calls=%async_computation.3 | async-start | bytes 6684672 | tf_op jit(solution)/shard_map/all_gather | solution.py:60
  8.6 216.8 %reduce-scatter.6.cloned.1.call-start = ((), (), s32[]{:S(2)}) async-start(), calls=%async_computation.6 | async-start | bytes 5308416 | tf_op jit(solution)/shard_map/reduce_scatter | solution.py:77
  76.5 4.0 copy-start.2
  77.2 2.4 copy-start
  140.4 14.6 %slice-start = ((s8[4718592]{0:T(1024)(128)(4,1)}), s8[4194304]{0:T(1024)(128)(4,1)S(1)}, s32[]{:S(2)}) async-start(s8[4718592]{0:T(1024)(128)(4,1)} %bitcast.100), calls=%async_computation.9 | async-start | bytes 8388608
  140.4 14.6 %slice-start.2 = ((s8[6291456]{0:T(1024)(128)(4,1)}), s8[4194304]{0:T(1024)(128)(4,1)S(1)}, s32[]{:S(2)}) async-start(s8[6291456]{0:T(1024)(128)(4,1)} %bitcast.113), calls=%async_computation.11 | async-start | bytes 8388608
  141.1 13.9 %copy-start.1 = (bf16[6,128,24,128]{3,2,1,0:T(8,128)(2,1)}, bf16[6,128,24,128]{3,2,1,0:T(8,128)(2,1)S(1)}, u32[]{:S(2)}) copy-start(bf16[6,128,24,128]{3,2,1,0:T(8,128)(2,1)S(1)} %broadcast_in_dim.44) | copy-start | bytes 14155780
  141.1 13.9 %slice-start.1 = ((s8[4718592]{0:T(1024)(128)(4,1)}), s8[524288]{0:T(1024)(128)(4,1)S(1)}, s32[]{:S(2)}) async-start(s8[4718592]{0:T(1024)(128)(4,1)} %bitcast.100), calls=%async_computation.10 | async-start | bytes 1048576
  141.1 13.9 %slice-start.3 = ((s8[6291456]{0:T(1024)(128)(4,1)}), s8[2097152]{0:T(1024)(128)(4,1)S(1)}, s32[]{:S(2)}) async-start(s8[6291456]{0:T(1024)(128)(4,1)} %bitcast.113), calls=%async_computation.12 | async-start | bytes 4194304
  169.1 0.7 copy-start.3
  169.1 115.5 %reduce-scatter.8.cloned.1.call-start = ((), (), s32[]{:S(2)}) async-start(), calls=%async_computation.7 | async-start | bytes 5308416 | tf_op jit(solution)/shard_map/reduce_scatter | solution.py:78
  188.0 203.2 %all-gather.8.cloned.1.call-start = ((), (), s32[]{:S(2)}) async-start(), calls=%async_computation.8 | async-start | bytes 10616832 | tf_op jit(solution)/shard_map/all_gather | solution.py:110
  289.3 1.8 copy-start.4
  290.4 193.8 %reduce-scatter.4.cloned.1.call-start = ((), (), s32[]{:S(2)}) async-start(), calls=%async_computation.5 | async-start | bytes 6684672 | tf_op jit(solution)/shard_map/reduce_scatter | solution.py:81
Sparse Core Ops, SparseCore 0:
  10.4 66.0 all-gather.5
  79.0 61.4 all-gather.3
  169.2 56.1 reduce-scatter.5
  227.7 56.9 reduce-scatter.7
  290.6 100.5 all-gather.7
  395.8 88.3 reduce-scatter.3
where the time goes:
time: 492 us; the launch traced here: 491 us
  waiting for transfers between devices  349 us (71%)
  local copies, waits for them, and re-layouts  54.8 us (11%)
  matrix products  52.6 us (11%)
  other arithmetic  20.2 us (4%)
  between operations  14.3 us (3%)
    all_gather x1, waiting for transfers between devices, shards(): all_steps = lax.all_gather(stacked, 'dp', axis=1, tiled=True)  89.2 us
    all_gather x1, waiting for transfers between devices, shards(): lax.all_gather(tokens_in, 'mp', axis=0, tiled=True)  64.2 us
    reduce_scatter x1, waiting for transfers between devices, shards(): lax.psum_scatter(lax.optimization_barrier(partial_term.astype(jnp.bfloat1...  63.7 us
    reduce_scatter x1, waiting for transfers between devices, shards(): lax.psum_scatter(down_sorted, 'dp', scatter_dimension=0, tiled=True)  59.2 us
    all_gather x1, waiting for transfers between devices, shards(): lax.all_gather(out_grad, 'mp', axis=0, tiled=True)  51.5 us
    reduce_scatter x1, waiting for transfers between devices, shards(): lax.psum_scatter(up_sorted, 'dp', scatter_dimension=0, tiled=True)  19.5 us
    dot_general x1, matrix products, shards(): jnp.einsum('td,fd->tf', grad_rows, down_live, preferred_element_type=jnp....  13.8 us
    gather x4, local copies, waits for them, and re-layouts, owned_rows(): matrix.reshape(buckets, bucket_rows, width)[chosen].astype(jnp.float32)  11.9 us
  transfers between devices with their start and end apart: 6, of which 6 were waited for; matrix products, arithmetic and copies ran while one was open for 18% of the time, Pallas kernels for 0%

commit v1 on v0

--- a/solution.py
+++ b/solution.py
@@ -55,10 +55,8 @@
     def owner_order(matrix, sorter):
         return matrix.reshape(buckets, bucket_rows, width)[sorter]
 
-    feat_rows, grad_rows = (
-        lax.all_gather(tokens_in, "mp", axis=0, tiled=True),
-        lax.all_gather(out_grad, "mp", axis=0, tiled=True),
-    )
+    both_rows = lax.all_gather(jnp.stack([tokens_in, out_grad]), "mp", axis=1, tiled=True)
+    feat_rows, grad_rows = both_rows[0], both_rows[1]
     hidden_pre = jnp.einsum("td,fd->tf", feat_rows, up_live, preferred_element_type=jnp.float32)
     activation, gelu_back = jax.vjp(jax.nn.gelu, hidden_pre)
     act_low = activation.astype(jnp.bfloat16)
@@ -73,10 +71,12 @@
         * keep_up
     ).astype(jnp.bfloat16)
     up_sorted = owner_order(grad_up, sorter_up)
-    up_summed, down_summed = (
-        lax.psum_scatter(up_sorted, "dp", scatter_dimension=0, tiled=True).astype(jnp.float32),
-        lax.psum_scatter(down_sorted, "dp", scatter_dimension=0, tiled=True).astype(jnp.float32),
+    by_owner = jnp.stack(
+        [up_sorted.reshape(owners, owned, bucket_rows, width), down_sorted.reshape(owners, owned, bucket_rows, width)],
+        axis=1,
     )
+    summed = lax.psum_scatter(by_owner, "dp", scatter_dimension=0, tiled=True).astype(jnp.float32)
+    up_summed, down_summed = summed[0, 0], summed[0, 1]
     partial_term = jnp.dot(hidden_grad, up_live, preferred_element_type=jnp.float32)
     input_grad = lax.psum_scatter(
         lax.optimization_barrier(partial_term.astype(jnp.bfloat16))

time: 492 us -> 480 us (0.976)
  waiting for transfers between devices: 349 us -> 322 us
  other arithmetic: 20.2 us -> 31.5 us
    all_gather x2 -> x1, waiting for transfers between devices: 116 us -> 88.6 us  [shards(): lax.all_gather(jnp.stack([tokens_in, out_grad]), 'mp', axis=1, tiled=True)]
    another operation x0 -> x2, other arithmetic: none -> 10.4 us  [the longest x1 8.38 us: shards(): jnp.stack([up_sorted.reshape(owners, owned, bucket_rows, width), down_sor...]
    reduce_scatter x2 -> x1, waiting for transfers between devices: 78.7 us -> 80.5 us  [shards(): lax.psum_scatter(by_owner, 'dp', scatter_dimension=0, tiled=True)]
  transfers between devices with their start and end apart: 6 -> 4, of which waited for: 6 -> 4; matrix products, arithmetic and copies ran while one was open for 18% -> 14% of each run, Pallas kernels for 0% -> 0%
where the time goes in v1:
time: 480 us; the launch traced here: 479 us
  waiting for transfers between devices  322 us (67%)
  local copies, waits for them, and re-layouts  56.8 us (12%)
  matrix products  54.3 us (11%)
  other arithmetic  31.5 us (7%)
  between operations  14 us (3%)
    all_gather x1, waiting for transfers between devices, shards(): all_steps = lax.all_gather(stacked, 'dp', axis=1, tiled=True)  89.3 us
    all_gather x1, waiting for transfers between devices, shards(): lax.all_gather(jnp.stack([tokens_in, out_grad]), 'mp', axis=1, tiled=True)  88.6 us
    reduce_scatter x1, waiting for transfers between devices, shards(): lax.psum_scatter(by_owner, 'dp', scatter_dimension=0, tiled=True)  80.5 us
    reduce_scatter x1, waiting for transfers between devices, shards(): lax.psum_scatter(lax.optimization_barrier(partial_term.astype(jnp.bfloat1...  63.7 us
    gather x4, local copies, waits for them, and re-layouts, owned_rows(): matrix.reshape(buckets, bucket_rows, width)[chosen].astype(jnp.float32)  14.2 us
    dot_general x1, matrix products, shards(): jnp.einsum('td,fd->tf', grad_rows, down_live, preferred_element_type=jnp....  13.2 us
    dot_general x1, matrix products, shards(): jnp.einsum('tf,td->fd', act_low, grad_rows, preferred_element_type=jnp.fl...  11.5 us
    gather x2, local copies, waits for them, and re-layouts, owner_order(): return matrix.reshape(buckets, bucket_rows, width)[sorter]  11 us
  transfers between devices with their start and end apart: 4, of which 4 were waited for; matrix products, arithmetic and copies ran while one was open for 14% of the time, Pallas kernels for 0%

profile of v1, /device:TPU:0, one launch (start us, length us, event | category | flops | bytes accessed | tf_op | source)
XLA Modules:
  0.0 479.2 jit_solution(1625153170130510813)
XLA Ops:
  7.2 0.0 all-gather.3.cloned.1.call-start
  7.2 2.1 pad_maximum_fusion.3
  9.3 0.0 all-gather.3.cloned.1.call-update
  9.3 0.0 reduce-scatter.5.cloned.1.call-start
  9.4 0.7 convert_element_type.101
  10.0 0.7 convert_element_type.100
  10.7 0.7 compare_select_fusion
  11.4 1.6 sort.32
  13.0 0.7 compare_select_fusion.1
  13.7 1.6 sort.31
  15.3 88.6 %all-gather.3.cloned.1.call-done = bf16[2,1024,3072]{2,1,0:T(8,128)(2,1)} async-done(((bf16[2,64,3072]{2,1,0:T(8,128)(2,1)}), bf16[2,1024,3072]{2,1,0:T(8,128)(2,1)}) %all-gather.3.cloned.1.call-update) | async-done | bytes 12582928 | tf_op jit(solution)/shard_map/all_gather | solution.py:58
  104.0 0.0 copy-start.4
  104.0 0.0 slice-start.2
  104.0 0.7 broadcast_in_dim.45
  104.6 0.0 copy-start
  104.6 3.3 copy-done.4
  108.0 0.0 slice-start.3
  108.0 8.6 %fusion.1 = f32[1024,768]{1,0:T(8,128)} fusion(bf16[2,1024,3072]{2,1,0:T(8,128)(2,1)} %all-gather.3.cloned.1.call-done, bf16[768,3072]{1,0:T(8,128)(2,1)S(1)} %copy-done.4, bf16[96,8,24,128]{3,2,1,0:T(8,128)(2,1)S(1)} %bitcast.105), kind=kOutput, calls=%fused_computation.16 | convolution fusion | flops 4834197504 | bytes 18874368 | tf_op jit(solution)/shard_map/td,fd->tf/dot_general | solution.py:60
  116.6 0.0 copy-done
  116.6 0.7 broadcast_in_dim.44
  117.3 0.0 copy-start.1
  117.3 0.0 slice-done.2
  117.3 0.0 slice-done.3
  117.3 0.0 slice-done.4
  117.4 11.5 %multiply_convert_fusion = bf16[768,3072]{1,0:T(8,128)(2,1)} fusion(bf16[2,1024,3072]{2,1,0:T(8,128)(2,1)S(1)} %bitcast.123, bf16[96,8,24,128]{3,2,1,0:T(8,128)(2,1)S(1)} %bitcast.110, f32[1024,768]{1,0:T(8,128)} %fusion.1), kind=kOutput, calls=%fused_computation.10 | convolution fusion | flops 4845993984 | bytes 18874368 | tf_op jit(solution)/shard_map/tf,td->fd/dot_general | solution.py:64
  128.9 0.0 copy-done.1
  128.9 5.5 %gather_fusion.2 = bf16[24,32,3072]{2,1,0:T(8,128)(2,1)} fusion(bf16[24,32,3072]{2,1,0:T(8,128)(2,1)} %bitcast.113, s32[1024]{0:T(1024)S(1)} %pad_clamp_fusion.3), kind=kCustom, calls=%fused_computation.2 | custom fusion | bytes 9437280 | tf_op jit(solution)/shard_map/gather | solution.py:56
  134.4 13.2 %fusion.9 = bf16[1024,768]{1,0:T(8,128)(2,1)S(1)} fusion(f32[1024,768]{1,0:T(8,128)} %fusion.1, bf16[768,3072]{1,0:T(8,128)(2,1)} %param.13, bf16[96,8,24,128]{3,2,1,0:T(8,128)(2,1)} %bitcast.111, bf16[2,1024,3072]{2,1,0:T(8,128)(2,1)} %all-gather.3.cloned.1.call-done), kind=kOutput, calls=%fused_computation.30 | convolution fusion | flops 4849926144 | bytes 20447232 | tf_op jit(solution)/shard_map/td,fd->tf/dot_general | solution.py:67
  147.6 0.0 slice-done
  147.7 0.0 slice-done.1
  147.7 0.0 copy-start.5
  147.7 10.2 %multiply_convert_fusion.1 = bf16[768,3072]{1,0:T(8,128)(2,1)} fusion(bf16[1024,768]{1,0:T(8,128)(2,1)S(1)} %fusion.9, bf16[2,1024,3072]{2,1,0:T(8,128)(2,1)} %all-gather.3.cloned.1.call-done, bf16[96,8,24,128]{3,2,1,0:T(8,128)(2,1)S(1)} %bitcast.109), kind=kOutput, calls=%fused_computation.11 | convolution fusion | flops 4838916096 | bytes 17301504 | tf_op jit(solution)/shard_map/tf,td->fd/dot_general | solution.py:70
  157.9 0.0 copy-done.5
  157.9 5.5 %gather_fusion.1 = bf16[24,32,3072]{2,1,0:T(8,128)(2,1)} fusion(bf16[24,32,3072]{2,1,0:T(8,128)(2,1)} %bitcast.112, s32[1024]{0:T(1024)S(1)} %pad_clamp_fusion.4), kind=kCustom, calls=%fused_computation.1 | custom fusion | bytes 9437280 | tf_op jit(solution)/shard_map/gather | solution.py:56
  163.4 8.4 %pad_maximum_fusion = bf16[8,2,3,32,3072]{4,3,2,1,0:T(8,128)(2,1)} fusion(bf16[8,1,3,32,3072]{4,3,2,1,0:T(8,128)(2,1)} %bitcast.101, bf16[8,1,3,32,3072]{4,3,2,1,0:T(8,128)(2,1)} %bitcast.103), kind=kLoop, calls=%fused_computation.8 | loop fusion | flops 4718592 | bytes 18874368 | tf_op jit(solution)/shard_map/stack | solution.py:74
  171.7 0.0 reduce-scatter.5.cloned.1.call-update
  171.8 0.3 all-gather.5.cloned.1.call-start
  172.0 0.1 broadcast_in_dim.46
  172.2 0.1 compare_select_fusion.2
  172.3 2.9 gather_fusion.3
  175.2 2.7 broadcast_in_dim.48
  177.9 3.6 gather_fusion
  181.5 0.1 broadcast_in_dim.52
  181.6 3.8 gather_fusion.5
  185.4 2.7 broadcast_in_dim.54
  188.1 3.9 gather_fusion.4
  192.0 80.5 %reduce-scatter.5.cloned.1.call-done = bf16[1,2,3,32,3072]{4,3,2,1,0:T(8,128)(2,1)} async-done(((bf16[8,2,3,32,3072]{4,3,2,1,0:T(8,128)(2,1)}), bf16[1,2,3,32,3072]{4,3,2,1,0:T(8,128)(2,1)}) %reduce-scatter.5.cloned.1.call-update) | async-done | bytes 1179664 | tf_op jit(solution)/shard_map/reduce_scatter | solution.py:78
  272.5 1.7 convert_element_type.111
  274.2 0.0 copy-done.2
  274.2 0.3 copy-done.3
  274.5 3.2 fusion.31
  277.7 0.0 copy-start.6
  277.7 1.1 pad_maximum_fusion.2
  278.8 0.0 all-gather.5.cloned.1.call-update
  278.8 0.0 reduce-scatter.3.cloned.1.call-start
  278.9 0.6 copy-done.6
  279.5 10.7 %convolution_convert_fusion = bf16[1024,3072]{1,0:T(8,128)(2,1)} fusion(bf16[1024,768]{1,0:T(8,128)(2,1)S(1)} %copy-done.6, bf16[768,3072]{1,0:T(8,128)(2,1)} %param.12, bf16[96,8,24,128]{3,2,1,0:T(8,128)(2,1)} %bitcast.106), kind=kOutput, calls=%fused_computation.14 | convolution fusion | flops 4837343232 | bytes 17301504 | tf_op jit(solution)/shard_map/dot_general | solution.py:80
  290.2 0.0 reduce-scatter.3.cloned.1.call-update
  290.3 89.3 %all-gather.5.cloned.1.call-done = bf16[2,24,32,3072]{3,2,1,0:T(8,128)(2,1)} async-done(((bf16[2,3,32,3072]{3,2,1,0:T(8,128)(2,1)}), bf16[2,24,32,3072]{3,2,1,0:T(8,128)(2,1)}) %all-gather.5.cloned.1.call-update) | async-done | bytes 9437200 | tf_op jit(solution)/shard_map/all_gather | solution.py:110
  379.6 9.0 %slice_bitcast_fusion.7 = (bf16[24,32,3072]{2,1,0:T(8,128)(2,1)}, bf16[24,32,3072]{2,1,0:T(8,128)(2,1)}) fusion(bf16[2,24,32,3072]{3,2,1,0:T(8,128)(2,1)} %all-gather.5.cloned.1.call-done), kind=kLoop, calls=%fused_computation.20 | loop fusion | bytes 18874368 | tf_op jit(solution)/shard_map/squeeze | solution.py:111
  388.5 5.5 %gather_fusion.7 = bf16[24,32,3072]{2,1,0:T(8,128)(2,1)} fusion(bf16[24,32,3072]{2,1,0:T(8,128)(2,1)} %get-tuple-element.11, s32[1024]{0:T(1024)S(1)} %pad_clamp_fusion), kind=kCustom, calls=%fused_computation.7 | custom fusion | bytes 9437280 | tf_op jit(solution)/shard_map/gather | solution.py:112
  394.0 5.9 %gather_fusion.6 = bf16[24,32,3072]{2,1,0:T(8,128)(2,1)} fusion(bf16[24,32,3072]{2,1,0:T(8,128)(2,1)} %get-tuple-element.10, s32[1024]{0:T(1024)S(1)} %pad_clamp_fusion.1), kind=kCustom, calls=%fused_computation.6 | custom fusion | bytes 9437280 | tf_op jit(solution)/shard_map/gather | solution.py:111
  399.9 9.1 %pad_maximum_fusion.1 = bf16[2,768,3072]{2,1,0:T(8,128)(2,1)} fusion(bf16[1,768,3072]{2,1,0:T(8,128)(2,1)} %bitcast.102, bf16[1,768,3072]{2,1,0:T(8,128)(2,1)} %bitcast.104), kind=kLoop, calls=%fused_computation.9 | loop fusion | flops 4718592 | bytes 18874368 | tf_op jit(solution)/shard_map/stack | solution.py:113
  408.9 63.7 %reduce-scatter.3.cloned.1.call-done = bf16[64,3072]{1,0:T(8,128)(2,1)} async-done(((bf16[1024,3072]{1,0:T(8,128)(2,1)}), bf16[64,3072]{1,0:T(8,128)(2,1)}) %reduce-scatter.3.cloned.1.call-update) | async-done | bytes 393232 | tf_op jit(solution)/shard_map/reduce_scatter | solution.py:81
  (19 shorter events, 0.1 us)
Async XLA Ops:
  7.2 96.8 %all-gather.3.cloned.1.call-start = ((), (), s32[]{:S(2)}) async-start(), calls=%async_computation.2 | async-start | bytes 13369344 | tf_op jit(solution)/shard_map/all_gather | solution.py:58
  9.3 263.2 %reduce-scatter.5.cloned.1.call-start = ((), (), s32[]{:S(2)}) async-start(), calls=%async_computation.4 | async-start | bytes 10616832 | tf_op jit(solution)/shard_map/reduce_scatter | solution.py:78
  104.0 4.0 copy-start.4
  104.0 13.4 %slice-start.2 = ((s8[12582912]{0:T(1024)(128)(4,1)}), s8[4194304]{0:T(1024)(128)(4,1)S(1)}, s32[]{:S(2)}) async-start(s8[12582912]{0:T(1024)(128)(4,1)} %bitcast.122), calls=%async_computation.8 | async-start | bytes 8388608
  104.6 12.0 %copy-start = (bf16[6,128,24,128]{3,2,1,0:T(8,128)(2,1)}, bf16[6,128,24,128]{3,2,1,0:T(8,128)(2,1)S(1)}, u32[]{:S(2)}) copy-start(bf16[6,128,24,128]{3,2,1,0:T(8,128)(2,1)S(1)} %broadcast_in_dim.45) | copy-start | bytes 14155780
  108.0 9.3 %slice-start.3 = ((s8[12582912]{0:T(1024)(128)(4,1)}), s8[4194304]{0:T(1024)(128)(4,1)S(1)}, s32[]{:S(2)}) async-start(s8[12582912]{0:T(1024)(128)(4,1)} %bitcast.122), calls=%async_computation.9 | async-start | bytes 8388608
  108.0 9.3 %slice-start.4 = ((s8[12582912]{0:T(1024)(128)(4,1)}), s8[4194304]{0:T(1024)(128)(4,1)S(1)}, s32[]{:S(2)}) async-start(s8[12582912]{0:T(1024)(128)(4,1)} %bitcast.122), calls=%async_computation.10 | async-start | bytes 8388608
  117.3 11.6 %copy-start.1 = (bf16[6,128,24,128]{3,2,1,0:T(8,128)(2,1)}, bf16[6,128,24,128]{3,2,1,0:T(8,128)(2,1)S(1)}, u32[]{:S(2)}) copy-start(bf16[6,128,24,128]{3,2,1,0:T(8,128)(2,1)S(1)} %broadcast_in_dim.44) | copy-start | bytes 14155780
  128.9 18.7 %slice-start = ((s8[4718592]{0:T(1024)(128)(4,1)}), s8[524288]{0:T(1024)(128)(4,1)S(1)}, s32[]{:S(2)}) async-start(s8[4718592]{0:T(1024)(128)(4,1)} %bitcast.107), calls=%async_computation.6 | async-start | bytes 1048576
  134.4 13.2 %slice-start.1 = ((s8[4718592]{0:T(1024)(128)(4,1)}), s8[4194304]{0:T(1024)(128)(4,1)S(1)}, s32[]{:S(2)}) async-start(s8[4718592]{0:T(1024)(128)(4,1)} %bitcast.107), calls=%async_computation.7 | async-start | bytes 8388608
  147.7 10.2 %copy-start.5 = (bf16[1024,768]{1,0:T(8,128)(2,1)}, bf16[1024,768]{1,0:T(8,128)(2,1)S(1)}, u32[]{:S(2)}) copy-start(bf16[1024,768]{1,0:T(8,128)(2,1)S(1)} %fusion.9) | copy-start | bytes 4718596
  171.8 207.8 %all-gather.5.cloned.1.call-start = ((), (), s32[]{:S(2)}) async-start(), calls=%async_computation.5 | async-start | bytes 10616832 | tf_op jit(solution)/shard_map/all_gather | solution.py:110
  188.1 86.1 %copy-start.2 = (f32[2,1,3,32,3072]{4,3,2,1,0:T(8,128)S(1)}, f32[2,1,3,32,3072]{4,3,2,1,0:T(8,128)}, u32[]{:S(2)}) copy-start(f32[2,1,3,32,3072]{4,3,2,1,0:T(8,128)} %param.19) | copy-start | bytes 7077892
  272.5 2.0 copy-start.3
  277.7 1.8 copy-start.6
  278.8 193.8 %reduce-scatter.3.cloned.1.call-start = ((), (), s32[]{:S(2)}) async-start(), calls=%async_computation.3 | async-start | bytes 6684672 | tf_op jit(solution)/shard_map/reduce_scatter | solution.py:81
Sparse Core Ops, SparseCore 0:
  11.0 92.8 all-gather.2
  171.9 100.5 reduce-scatter.4
  279.0 100.5 all-gather.4
  384.2 88.4 reduce-scatter.2

commit v2 on v1

v2 whole, which is shorter than its diff:
```python
import jax
import jax.numpy as jnp
from jax import lax
from jax.sharding import PartitionSpec as P


bias_first = 1.0 - 0.9**10
bias_second = 1.0 - 0.95**10


def expand_mask(blocks):
    block_rows, block_cols = blocks.shape
    wide = jnp.broadcast_to(
        blocks.astype(jnp.bfloat16)[:, None, :, None], (block_rows, 128, block_cols, 128)
    )
    return wide.reshape(block_rows * 128, block_cols * 128)


def adam_step(summed, moment_a, moment_b, weight_rows, mask_rows):
    first_new = 0.9 * moment_a + 0.1 * summed
    second_new = 0.95 * moment_b + 0.05 * summed * summed
    update = first_new / bias_first / (jnp.sqrt(second_new / bias_second) + 1e-08)
    return (mask_rows * (update + 0.1 * weight_rows)).astype(jnp.bfloat16)


def slot_places(order_table, owners, owned):
    return order_table % owners * owned + order_table // owners


def layer(
    tokens_in,
    out_grad,
    w_up,
    w_down,
    mask_up,
    mask_down,
    order_up,
    order_down,
    moment_one,
    moment_two,
):
    owners = lax.axis_size("dp")
    hidden_local, width = w_up.shape
    buckets = order_up.shape[0]
    owned = buckets // owners
    bucket_rows = hidden_local // buckets
    local_rows = tokens_in.shape[0]
    half = local_rows // 2
    place_up = slot_places(order_up, owners, owned)
    place_down = slot_places(order_down, owners, owned)
    sorter_up = jnp.argsort(place_up)
    sorter_down = jnp.argsort(place_down)

    def owner_order(matrix, sorter):
        return matrix.reshape(buckets, bucket_rows, width)[sorter].reshape(hidden_local, width)

    keep_up = owner_order(expand_mask(mask_up), sorter_up)
    keep_down = owner_order(expand_mask(mask_down), sorter_up)
    w_up_s = owner_order(w_up, sorter_up)
    w_down_s = owner_order(w_down, sorter_up)
    up_live = w_up_s * keep_up
    down_live = w_down_s * keep_down
    down_from_up = jnp.argsort(sorter_up)[sorter_down]

    def gather_rows(lo):
        both = jnp.stack([tokens_in[lo : lo + half], out_grad[lo : lo + half]])
        rows = lax.all_gather(both, "mp", axis=1, tiled=True)
        return rows[0], rows[1]

    def piece(feat_rows, grad_rows):
      hidden_pre = jnp.einsum("td,fd->tf", feat_rows, up_live, preferred_element_type=jnp.float32)
      activation, gelu_back = jax.vjp(jax.nn.gelu, hidden_pre)
      act_low = activation.astype(jnp.bfloat16)
      down_part = jnp.einsum("tf,td->fd", act_low, grad_rows, preferred_element_type=jnp.float32)
      act_grad = jnp.einsum("td,fd->tf", grad_rows, down_live, preferred_element_type=jnp.float32)
      hidden_grad = gelu_back(act_grad)[0].astype(jnp.bfloat16)
      up_part = jnp.einsum("tf,td->fd", hidden_grad, feat_rows, preferred_element_type=jnp.float32)
      partial_term = jnp.dot(hidden_grad, up_live, preferred_element_type=jnp.float32)
      input_part = lax.psum_scatter(
          lax.optimization_barrier(partial_term.astype(jnp.bfloat16))
          .astype(jnp.float32)
          .astype(jnp.bfloat16),
          "mp",
          scatter_dimension=0,
          tiled=True,
      )
      return up_part, down_part, input_part

    feat_a, grad_a = gather_rows(0)
    feat_b, grad_b = gather_rows(half)
    up_a, down_a, input_a = piece(feat_a, grad_a)
    up_b, down_b, input_b = piece(feat_b, grad_b)
    grad_up = ((up_a + up_b) * keep_up).astype(jnp.bfloat16)
    grad_down = ((down_a + down_b) * keep_down).astype(jnp.bfloat16)

    by_owner = jnp.stack(
        [
            grad_up.reshape(owners, owned, bucket_rows, width),
            grad_down.reshape(buckets, bucket_rows, width)[down_from_up].reshape(owners, owned, bucket_rows, width),
        ],
        axis=1,
    )
    summed = lax.psum_scatter(by_owner, "dp", scatter_dimension=0, tiled=True).astype(jnp.float32)
    up_summed, down_summed = summed[0, 0], summed[0, 1]
    owner_index = lax.axis_index("dp")

    def owned_rows(matrix, sorter):
        chosen = lax.dynamic_slice_in_dim(sorter, owner_index * owned, owned, 0)
        return matrix.reshape(buckets, bucket_rows, width)[chosen].astype(jnp.float32)

    step_up = adam_step(
        up_summed,
        moment_one[0, 0],
        moment_two[0, 0],
        owned_rows(w_up, sorter_up),
        owned_rows(expand_mask(mask_up), sorter_up),
    )
    step_down = adam_step(
        down_summed,
        moment_one[1, 0],
        moment_two[1, 0],
        owned_rows(w_down, sorter_down),
        owned_rows(expand_mask(mask_down), sorter_down),
    )
    stacked = jnp.stack([step_up, step_down])
    all_steps = lax.all_gather(stacked, "dp", axis=1, tiled=True)
    update_up = all_steps[0][place_up].reshape(hidden_local, width)
    update_down = all_steps[1][place_down].reshape(hidden_local, width)
    input_grad = jnp.concatenate([input_a, input_b], axis=0)
    return (input_grad, jnp.stack([update_up, update_down]))


def solution(mesh):
    placed = (
        P(("dp", "mp"), None),
        P(("dp", "mp"), None),
        P("mp", None),
        P("mp", None),
        P("mp", None),
        P("mp", None),
        P(),
        P(),
        P(None, "mp", "dp", None, None),
        P(None, "mp", "dp", None, None),
    )
    return jax.shard_map(
        layer,
        mesh=mesh,
        in_specs=placed,
        out_specs=(P(("dp", "mp"), None), P(None, "mp", None)),
        check_vma=False,
    )
```

time: 480 us -> 591 us (1.23)
  waiting for transfers between devices: 322 us -> 402 us
  local copies, waits for them, and re-layouts: 56.8 us -> 72 us
  other arithmetic: 31.5 us -> 43.8 us
    reduce_scatter x2 -> x3, waiting for transfers between devices: 144 us -> 222 us  [the longest x2 150 us: piece(): lax.psum_scatter(lax.optimization_barrier(partial_term.astype(jnp.bfloat1...]
    gather x4 -> x8, local copies, waits for them, and re-layouts: 22.3 us -> 39.3 us  [the longest x4 22.1 us: owner_order(): matrix.reshape(buckets, bucket_rows, width)[sorter]]
    mul x0 -> x2, other arithmetic: none -> 12.7 us  [the longest x1 8.46 us: layer(): up_live = w_up_s * keep_up]
    dot_general x5 -> x10, matrix products: 54.3 us -> 57.7 us  [the longest x2 14.6 us: piece(): jnp.einsum('td,fd->tf', grad_rows, down_live, preferred_element_type=jnp....]
    all_gather x2 -> x3, waiting for transfers between devices: 178 us -> 180 us  [the longest x1 101 us: layer(): all_steps = lax.all_gather(stacked, 'dp', axis=1, tiled=True)]
    another operation x4 -> x5, other arithmetic: 20.6 us -> 19.4 us  [the longest x1 8.38 us: layer(): jnp.stack([grad_up.reshape(owners, owned, bucket_rows, width), grad_down....]
  transfers between devices with their start and end apart: 4 -> 6, of which waited for: 4 -> 6; matrix products, arithmetic and copies ran while one was open for 14% -> 15% of each run, Pallas kernels for 0% -> 0%
where the time goes in v2:
time: 591 us; the launch traced here: 590 us
  waiting for transfers between devices  402 us (68%)
  local copies, waits for them, and re-layouts  72 us (12%)
  matrix products  57.7 us (10%)
  other arithmetic  43.8 us (7%)
  between operations  14.5 us (2%)
    reduce_scatter x2, waiting for transfers between devices, piece(): lax.psum_scatter(lax.optimization_barrier(partial_term.astype(jnp.bfloat1...  150 us
    all_gather x1, waiting for transfers between devices, layer(): all_steps = lax.all_gather(stacked, 'dp', axis=1, tiled=True)  101 us
    all_gather x2, waiting for transfers between devices, gather_rows(): rows = lax.all_gather(both, 'mp', axis=1, tiled=True)  78.8 us
    reduce_scatter x1, waiting for transfers between devices, layer(): lax.psum_scatter(by_owner, 'dp', scatter_dimension=0, tiled=True)  71.8 us
    gather x4, local copies, waits for them, and re-layouts, owner_order(): matrix.reshape(buckets, bucket_rows, width)[sorter]  22.1 us
    dot_general x2, matrix products, piece(): jnp.einsum('td,fd->tf', grad_rows, down_live, preferred_element_type=jnp....  14.6 us
    gather x4, local copies, waits for them, and re-layouts, owned_rows(): matrix.reshape(buckets, bucket_rows, width)[chosen].astype(jnp.float32)  13.8 us
    dot_general x2, matrix products, piece(): jnp.dot(hidden_grad, up_live, preferred_element_type=jnp.float32)  12.7 us
  transfers between devices with their start and end apart: 6, of which 6 were waited for; matrix products, arithmetic and copies ran while one was open for 15% of the time, Pallas kernels for 0%

profile of v2, /device:TPU:0, one launch (start us, length us, event | category | flops | bytes accessed | tf_op | source)
XLA Modules:
  0.0 589.8 jit_solution(5144078158090168020)
XLA Ops:
  7.2 0.0 all-gather.6.cloned.1.call-start
  7.2 1.3 slice_bitcast_fusion.22
  8.5 0.8 pad_maximum_fusion.4
  9.3 0.0 all-gather.6.cloned.1.call-update
  9.3 0.0 all-gather.4.cloned.1.call-start
  9.4 0.8 pad_maximum_fusion.3
  10.2 0.0 all-gather.4.cloned.1.call-update
  10.2 0.0 reduce-scatter.8.cloned.1.call-start
  10.3 0.1 broadcast_in_dim.25
  10.4 0.1 broadcast_in_dim.56
  10.6 1.6 sort.45
  12.2 1.6 sort.46
  13.8 2.7 broadcast_in_dim.58
  16.5 5.6 gather_fusion.3
  22.1 2.7 broadcast_in_dim.27
  24.8 5.5 gather_fusion.1
  30.3 5.5 gather_fusion.2
  35.8 5.5 gather_fusion
  41.3 1.6 sort.47
  43.0 0.7 gather_fusion.5
  43.7 8.5 %mul.292 = bf16[24,32,3072]{2,1,0:T(8,128)(2,1)} multiply(bf16[24,32,3072]{2,1,0:T(8,128)(2,1)} %gather_fusion.2, bf16[24,32,3072]{2,1,0:T(8,128)(2,1)} %gather_fusion.3) | non-fusion elementwise | flops 2359296 | bytes 14155776 | tf_op jit(solution)/shard_map/mul | solution.py:61
  52.2 4.2 mul.290
  56.4 20.8 %all-gather.6.cloned.1.call-done = bf16[2,512,3072]{2,1,0:T(8,128)(2,1)} async-done(((bf16[2,32,3072]{2,1,0:T(8,128)(2,1)}), bf16[2,512,3072]{2,1,0:T(8,128)(2,1)}) %all-gather.6.cloned.1.call-update) | async-done | bytes 6291472 | tf_op jit(solution)/shard_map/all_gather | solution.py:67
  77.2 5.9 %fusion.7 = f32[512,768]{1,0:T(8,128)S(1)} fusion(bf16[768,3072]{1,0:T(8,128)(2,1)} %bitcast.138, bf16[2,512,3072]{2,1,0:T(8,128)(2,1)} %all-gather.6.cloned.1.call-done), kind=kOutput, calls=%fused_computation.31 | convolution fusion | flops 2415919104 | bytes 9437184 | tf_op jit(solution)/shard_map/td,fd->tf/dot_general | solution.py:71
  83.1 58.0 %all-gather.4.cloned.1.call-done = bf16[2,512,3072]{2,1,0:T(8,128)(2,1)} async-done(((bf16[2,32,3072]{2,1,0:T(8,128)(2,1)}), bf16[2,512,3072]{2,1,0:T(8,128)(2,1)}) %all-gather.4.cloned.1.call-update) | async-done | bytes 6291472 | tf_op jit(solution)/shard_map/all_gather | solution.py:67
  141.2 6.1 %fusion.5 = f32[512,768]{1,0:T(8,128)S(1)} fusion(bf16[768,3072]{1,0:T(8,128)(2,1)} %bitcast.139, bf16[2,512,3072]{2,1,0:T(8,128)(2,1)} %all-gather.4.cloned.1.call-done), kind=kOutput, calls=%fused_computation.29 | convolution fusion | flops 2415919104 | bytes 9437184 | tf_op jit(solution)/shard_map/td,fd->tf/dot_general | solution.py:71
  147.3 3.0 fusion.2
  150.3 0.3 copy-done.1
  150.6 6.7 %fusion = bf16[768,3072]{1,0:T(8,128)(2,1)} fusion(bf16[768,3072]{1,0:T(8,128)(2,1)} %bitcast.124, f32[768,3072]{1,0:T(8,128)S(1)} %fusion.2, bf16[2,512,3072]{2,1,0:T(8,128)(2,1)S(1)} %copy-done.1, f32[512,768]{1,0:T(8,128)S(1)} %fusion.7), kind=kOutput, calls=%fused_computation.15 | convolution fusion | flops 2428895232 | bytes 23592960 | tf_op jit(solution)/shard_map/tf,td->fd/dot_general | solution.py:74
  157.4 5.5 gather_fusion.6
  162.8 7.7 %fusion.21 = bf16[512,768]{1,0:T(8,128)(2,1)} fusion(f32[512,768]{1,0:T(8,128)S(1)} %fusion.7, bf16[768,3072]{1,0:T(8,128)(2,1)} %bitcast.142, bf16[2,512,3072]{2,1,0:T(8,128)(2,1)} %all-gather.6.cloned.1.call-done), kind=kOutput, calls=%fused_computation.51 | convolution fusion | flops 2423783424 | bytes 10223616 | tf_op jit(solution)/shard_map/td,fd->tf/dot_general | solution.py:75
  170.6 6.9 %fusion.14 = bf16[512,768]{1,0:T(8,128)(2,1)S(1)} fusion(f32[512,768]{1,0:T(8,128)S(1)} %copy-done.13, bf16[768,3072]{1,0:T(8,128)(2,1)} %bitcast.143, bf16[2,512,3072]{2,1,0:T(8,128)(2,1)} %all-gather.4.cloned.1.call-done), kind=kOutput, calls=%fused_computation.44 | convolution fusion | flops 2423783424 | bytes 10223616 | tf_op jit(solution)/shard_map/td,fd->tf/dot_general | solution.py:75
  177.5 2.7 fusion.4
  180.2 5.9 %fusion.1 = bf16[768,3072]{1,0:T(8,128)(2,1)} fusion(bf16[768,3072]{1,0:T(8,128)(2,1)S(1)} %bitcast.123, f32[768,3072]{1,0:T(8,128)S(1)} %fusion.4, bf16[512,768]{1,0:T(8,128)(2,1)} %fusion.21, bf16[2,512,3072]{2,1,0:T(8,128)(2,1)S(1)} %bitcast.133), kind=kOutput, calls=%fused_computation.17 | convolution fusion | flops 2425356288 | bytes 22806528 | tf_op jit(solution)/shard_map/tf,td->fd/dot_general | solution.py:77
  186.2 8.4 %pad_maximum_fusion = bf16[8,2,3,32,3072]{4,3,2,1,0:T(8,128)(2,1)} fusion(bf16[8,1,3,32,3072]{4,3,2,1,0:T(8,128)(2,1)} %bitcast.127, bf16[8,1,3,32,3072]{4,3,2,1,0:T(8,128)(2,1)} %bitcast.131), kind=kLoop, calls=%fused_computation.12 | loop fusion | flops 4718592 | bytes 18874368 | tf_op jit(solution)/shard_map/stack | solution.py:96
  194.6 0.0 reduce-scatter.8.cloned.1.call-update
  194.6 0.0 reduce-scatter.4.cloned.1.call-start
  194.6 1.1 copy-done.11
  195.7 6.3 %convolution_convert_fusion.1 = bf16[512,3072]{1,0:T(8,128)(2,1)} fusion(bf16[512,768]{1,0:T(8,128)(2,1)S(1)} %copy-done.11, bf16[768,3072]{1,0:T(8,128)(2,1)} %bitcast.140), kind=kOutput, calls=%fused_computation.21 | convolution fusion | flops 2417491968 | bytes 8650752 | tf_op jit(solution)/shard_map/dot_general | solution.py:78
  202.0 0.0 reduce-scatter.4.cloned.1.call-update
  202.0 0.0 reduce-scatter.6.cloned.1.call-start
  202.1 1.1 copy-done.4
  203.2 6.4 %convolution_convert_fusion = bf16[512,3072]{1,0:T(8,128)(2,1)} fusion(bf16[512,768]{1,0:T(8,128)(2,1)S(1)} %copy-done.4, bf16[768,3072]{1,0:T(8,128)(2,1)} %bitcast.141), kind=kOutput, calls=%fused_computation.20 | convolution fusion | flops 2417491968 | bytes 8650752 | tf_op jit(solution)/shard_map/dot_general | solution.py:78
  209.6 0.0 reduce-scatter.6.cloned.1.call-update
  209.6 0.0 all-gather.8.cloned.1.call-start
  209.6 0.1 compare_select_fusion.2
  209.7 3.0 gather_fusion.7
  212.8 3.0 gather_fusion.4
  215.8 3.9 gather_fusion.9
  219.7 3.9 gather_fusion.8
  223.6 71.8 %reduce-scatter.8.cloned.1.call-done = bf16[1,2,3,32,3072]{4,3,2,1,0:T(8,128)(2,1)} async-done(((bf16[8,2,3,32,3072]{4,3,2,1,0:T(8,128)(2,1)}), bf16[1,2,3,32,3072]{4,3,2,1,0:T(8,128)(2,1)}) %reduce-scatter.8.cloned.1.call-update) | async-done | bytes 1179664 | tf_op jit(solution)/shard_map/reduce_scatter | solution.py:103
  295.4 1.7 convert_element_type.135
  297.1 0.3 copy-done.3
  297.4 3.2 fusion.39
  300.6 1.1 pad_maximum_fusion.2
  301.7 0.0 all-gather.8.cloned.1.call-update
  301.8 71.6 %reduce-scatter.4.cloned.1.call-done = bf16[32,3072]{1,0:T(8,128)(2,1)} async-done(((bf16[512,3072]{1,0:T(8,128)(2,1)}), bf16[32,3072]{1,0:T(8,128)(2,1)}) %reduce-scatter.4.cloned.1.call-update) | async-done | bytes 196624 | tf_op jit(solution)/shard_map/reduce_scatter | solution.py:79
  373.4 78.2 %reduce-scatter.6.cloned.1.call-done = bf16[32,3072]{1,0:T(8,128)(2,1)} async-done(((bf16[512,3072]{1,0:T(8,128)(2,1)}), bf16[32,3072]{1,0:T(8,128)(2,1)}) %reduce-scatter.6.cloned.1.call-update) | async-done | bytes 196624 | tf_op jit(solution)/shard_map/reduce_scatter | solution.py:79
  451.6 1.8 pad_maximum_fusion.5
  453.4 101.1 %all-gather.8.cloned.1.call-done = bf16[2,24,32,3072]{3,2,1,0:T(8,128)(2,1)} async-done(((bf16[2,3,32,3072]{3,2,1,0:T(8,128)(2,1)}), bf16[2,24,32,3072]{3,2,1,0:T(8,128)(2,1)}) %all-gather.8.cloned.1.call-update) | async-done | bytes 9437200 | tf_op jit(solution)/shard_map/all_gather | solution.py:126
  554.5 9.1 %slice_bitcast_fusion.1 = (bf16[24,32,3072]{2,1,0:T(8,128)(2,1)}, bf16[24,32,3072]{2,1,0:T(8,128)(2,1)}) fusion(bf16[2,24,32,3072]{3,2,1,0:T(8,128)(2,1)} %all-gather.8.cloned.1.call-done), kind=kLoop, calls=%fused_computation.19 | loop fusion | bytes 18874368 | tf_op jit(solution)/shard_map/squeeze | solution.py:127
  563.6 5.5 gather_fusion.10
  569.1 5.5 gather_fusion.11
  574.6 8.4 %pad_maximum_fusion.1 = bf16[2,768,3072]{2,1,0:T(8,128)(2,1)} fusion(bf16[1,768,3072]{2,1,0:T(8,128)(2,1)} %bitcast.130, bf16[1,768,3072]{2,1,0:T(8,128)(2,1)} %bitcast.128), kind=kLoop, calls=%fused_computation.13 | loop fusion | flops 4718592 | bytes 18874368 | tf_op jit(solution)/shard_map/stack | solution.py:130
  (63 shorter events, 0.2 us)
Async XLA Ops:
  7.2 3.1 copy-start.5
  7.2 3.1 copy-start.6
  7.2 3.3 copy-start.8
  7.2 70.0 %all-gather.6.cloned.1.call-start = ((), (), s32[]{:S(2)}) async-start(), calls=%async_computation.5 | async-start | bytes 6684672 | tf_op jit(solution)/shard_map/all_gather | solution.py:67
  9.3 131.8 %all-gather.4.cloned.1.call-start = ((), (), s32[]{:S(2)}) async-start(), calls=%async_computation.3 | async-start | bytes 6684672 | tf_op jit(solution)/shard_map/all_gather | solution.py:67
  10.2 285.2 %reduce-scatter.8.cloned.1.call-start = ((), (), s32[]{:S(2)}) async-start(), calls=%async_computation.7 | async-start | bytes 10616832 | tf_op jit(solution)/shard_map/reduce_scatter | solution.py:103
  35.8 5.5 copy-start.9
  43.0 9.2 %slice-start.2 = ((s8[4718592]{0:T(1024)(128)(4,1)}), s8[524288]{0:T(1024)(128)(4,1)S(1)}, s32[]{:S(2)}) async-start(s8[4718592]{0:T(1024)(128)(4,1)} %bitcast.125), calls=%async_computation.11 | async-start | bytes 1048576
  43.7 8.5 %slice-start.3 = ((s8[4718592]{0:T(1024)(128)(4,1)}), s8[4194304]{0:T(1024)(128)(4,1)S(1)}, s32[]{:S(2)}) async-start(s8[4718592]{0:T(1024)(128)(4,1)} %bitcast.125), calls=%async_computation.12 | async-start | bytes 8388608
  43.7 8.5 %copy-start = (bf16[24,32,3072]{2,1,0:T(8,128)(2,1)S(1)}, bf16[24,32,3072]{2,1,0:T(8,128)(2,1)}, u32[]{:S(2)}) copy-start(bf16[24,32,3072]{2,1,0:T(8,128)(2,1)} %gather_fusion) | copy-start | bytes 14155780
  141.2 6.1 %copy-start.7 = (bf16[2,512,3072]{2,1,0:T(8,128)(2,1)S(1)}, bf16[2,512,3072]{2,1,0:T(8,128)(2,1)}, u32[]{:S(2)}) copy-start(bf16[2,512,3072]{2,1,0:T(8,128)(2,1)} %all-gather.4.cloned.1.call-done) | copy-start | bytes 18874372
  147.2 3.0 copy-start.12
  147.2 3.4 copy-start.1
  162.8 7.8 %copy-start.13 = (f32[512,768]{1,0:T(8,128)S(1)}, f32[512,768]{1,0:T(8,128)}, u32[]{:S(2)}) copy-start(f32[512,768]{1,0:T(8,128)} %copy-done.12) | copy-start | bytes 4718596
  162.8 14.6 %slice-start.6 = ((s8[6291456]{0:T(1024)(128)(4,1)}), s8[4194304]{0:T(1024)(128)(4,1)S(1)}, s32[]{:S(2)}) async-start(s8[6291456]{0:T(1024)(128)(4,1)} %bitcast.148), calls=%async_computation.15 | async-start | bytes 8388608
  162.8 17.4 %slice-start = ((s8[4718592]{0:T(1024)(128)(4,1)}), s8[4194304]{0:T(1024)(128)(4,1)S(1)}, s32[]{:S(2)}) async-start(s8[4718592]{0:T(1024)(128)(4,1)} %bitcast.121), calls=%async_computation.9 | async-start | bytes 8388608
  162.8 17.4 %slice-start.4 = ((s8[6291456]{0:T(1024)(128)(4,1)}), s8[4194304]{0:T(1024)(128)(4,1)S(1)}, s32[]{:S(2)}) async-start(s8[6291456]{0:T(1024)(128)(4,1)} %bitcast.132), calls=%async_computation.13 | async-start | bytes 8388608
  170.6 6.9 %slice-start.7 = ((s8[6291456]{0:T(1024)(128)(4,1)}), s8[2097152]{0:T(1024)(128)(4,1)S(1)}, s32[]{:S(2)}) async-start(s8[6291456]{0:T(1024)(128)(4,1)} %bitcast.148), calls=%async_computation.16 | async-start | bytes 4194304
  170.6 9.6 %slice-start.1 = ((s8[4718592]{0:T(1024)(128)(4,1)}), s8[524288]{0:T(1024)(128)(4,1)S(1)}, s32[]{:S(2)}) async-start(s8[4718592]{0:T(1024)(128)(4,1)} %bitcast.121), calls=%async_computation.10 | async-start | bytes 1048576
  170.6 9.6 %slice-start.5 = ((s8[6291456]{0:T(1024)(128)(4,1)}), s8[2097152]{0:T(1024)(128)(4,1)S(1)}, s32[]{:S(2)}) async-start(s8[6291456]{0:T(1024)(128)(4,1)} %bitcast.132), calls=%async_computation.14 | async-start | bytes 4194304
  177.5 2.7 copy-start.10
  194.6 1.1 copy-start.11
  194.6 178.8 %reduce-scatter.4.cloned.1.call-start = ((), (), s32[]{:S(2)}) async-start(), calls=%async_computation.4 | async-start | bytes 3342336 | tf_op jit(solution)/shard_map/reduce_scatter | solution.py:79
  202.0 1.2 copy-start.4
  202.0 249.6 %reduce-scatter.6.cloned.1.call-start = ((), (), s32[]{:S(2)}) async-start(), calls=%async_computation.6 | async-start | bytes 3342336 | tf_op jit(solution)/shard_map/reduce_scatter | solution.py:79
  209.6 344.9 %all-gather.8.cloned.1.call-start = ((), (), s32[]{:S(2)}) async-start(), calls=%async_computation.8 | async-start | bytes 10616832 | tf_op jit(solution)/shard_map/all_gather | solution.py:126
  219.7 77.4 %copy-start.2 = (f32[2,1,3,32,3072]{4,3,2,1,0:T(8,128)S(1)}, f32[2,1,3,32,3072]{4,3,2,1,0:T(8,128)}, u32[]{:S(2)}) copy-start(f32[2,1,3,32,3072]{4,3,2,1,0:T(8,128)} %param.19) | copy-start | bytes 7077892
  295.4 2.0 copy-start.3
Sparse Core Ops, SparseCore 0:
  11.1 66.0 all-gather.5
  79.7 61.4 all-gather.3
  194.7 100.6 reduce-scatter.7
  299.3 74.0 reduce-scatter.3
  377.3 74.2 reduce-scatter.5
  453.7 100.7 all-gather.7

commit v3 on v1

--- a/solution.py
+++ b/solution.py
@@ -2,6 +2,7 @@
 import jax.numpy as jnp
 from jax import lax
 from jax.sharding import PartitionSpec as P
+
 
 bias_first = 1.0 - 0.9**10
 bias_second = 1.0 - 0.95**10
@@ -26,7 +27,7 @@
     return order_table % owners * owned + order_table // owners
 
 
-def shards(
+def layer(
     tokens_in,
     out_grad,
     w_up,
@@ -71,12 +72,8 @@
         * keep_up
     ).astype(jnp.bfloat16)
     up_sorted = owner_order(grad_up, sorter_up)
-    by_owner = jnp.stack(
-        [up_sorted.reshape(owners, owned, bucket_rows, width), down_sorted.reshape(owners, owned, bucket_rows, width)],
-        axis=1,
-    )
-    summed = lax.psum_scatter(by_owner, "dp", scatter_dimension=0, tiled=True).astype(jnp.float32)
-    up_summed, down_summed = summed[0, 0], summed[0, 1]
+    down_summed = lax.psum_scatter(down_sorted, "dp", scatter_dimension=0, tiled=True).astype(jnp.float32)
+    up_summed = lax.psum_scatter(up_sorted, "dp", scatter_dimension=0, tiled=True).astype(jnp.float32)
     partial_term = jnp.dot(hidden_grad, up_live, preferred_element_type=jnp.float32)
     input_grad = lax.psum_scatter(
         lax.optimization_barrier(partial_term.astype(jnp.bfloat16))
@@ -127,7 +124,7 @@
         P(None, "mp", "dp", None, None),
     )
     return jax.shard_map(
-        shards,
+        layer,
         mesh=mesh,
         in_specs=placed,
         out_specs=(P(("dp", "mp"), None), P(None, "mp", None)),

time: 480 us -> 468 us (0.975)
  other arithmetic: 31.5 us -> 22.3 us
  local copies, waits for them, and re-layouts: 56.8 us -> 51.4 us
    convert_element_type x2 -> x0, other arithmetic: 4.83 us -> none  [the longest x1 3.17 us: adam_step(): return (mask_rows * (update + 0.1 * weight_rows)).astype(jnp.bfloat16)]
    reduce_scatter x2 -> x3, waiting for transfers between devices: 144 us -> 142 us  [the longest x1 63.7 us: layer(): lax.psum_scatter(lax.optimization_barrier(partial_term.astype(jnp.bfloat1...]
  transfers between devices with their start and end apart: 4 -> 5, of which waited for: 4 -> 5; matrix products, arithmetic and copies ran while one was open for 14% -> 17% of each run, Pallas kernels for 0% -> 0%
where the time goes in v3:
time: 468 us; the launch traced here: 467 us
  waiting for transfers between devices  322 us (69%)
  matrix products  57.3 us (12%)
  local copies, waits for them, and re-layouts  51.4 us (11%)
  other arithmetic  22.3 us (5%)
  between operations  14 us (3%)
    all_gather x1, waiting for transfers between devices, layer(): lax.all_gather(jnp.stack([tokens_in, out_grad]), 'mp', axis=1, tiled=True)  90.9 us
    all_gather x1, waiting for transfers between devices, layer(): all_steps = lax.all_gather(stacked, 'dp', axis=1, tiled=True)  89.3 us
    reduce_scatter x1, waiting for transfers between devices, layer(): lax.psum_scatter(lax.optimization_barrier(partial_term.astype(jnp.bfloat1...  63.7 us
    reduce_scatter x1, waiting for transfers between devices, layer(): lax.psum_scatter(down_sorted, 'dp', scatter_dimension=0, tiled=True)  59.4 us
    reduce_scatter x1, waiting for transfers between devices, layer(): lax.psum_scatter(up_sorted, 'dp', scatter_dimension=0, tiled=True)  18.8 us
    dot_general x1, matrix products, layer(): jnp.einsum('td,fd->tf', grad_rows, down_live, preferred_element_type=jnp....  13.3 us
    gather x4, local copies, waits for them, and re-layouts, owned_rows(): matrix.reshape(buckets, bucket_rows, width)[chosen].astype(jnp.float32)  11.9 us
    dot_general x1, matrix products, layer(): jnp.einsum('td,fd->tf', feat_rows, up_live, preferred_element_type=jnp.fl...  11.8 us
  transfers between devices with their start and end apart: 5, of which 5 were waited for; matrix products, arithmetic and copies ran while one was open for 17% of the time, Pallas kernels for 0%

profile of v3, /device:TPU:0, one launch (start us, length us, event | category | flops | bytes accessed | tf_op | source)
XLA Modules:
  0.0 467.4 jit_solution(9633476465454146021)
XLA Ops:
  7.2 0.0 all-gather.3.cloned.1.call-start
  7.2 2.1 pad_maximum_fusion.2
  9.3 0.0 all-gather.3.cloned.1.call-update
  9.3 0.0 reduce-scatter.6.cloned.1.call-start
  9.4 0.7 convert_element_type.54
  10.0 0.7 convert_element_type.53
  10.7 0.7 compare_select_fusion.1
  11.4 1.6 sort.31
  13.0 90.9 %all-gather.3.cloned.1.call-done = bf16[2,1024,3072]{2,1,0:T(8,128)(2,1)} async-done(((bf16[2,64,3072]{2,1,0:T(8,128)(2,1)}), bf16[2,1024,3072]{2,1,0:T(8,128)(2,1)}) %all-gather.3.cloned.1.call-update) | async-done | bytes 12582928 | tf_op jit(solution)/shard_map/all_gather | solution.py:59
  104.0 0.0 slice-start
  104.0 0.7 broadcast_in_dim.45
  104.6 0.0 copy-start
  104.6 0.0 slice-start.1
  104.7 11.8 %fusion.1 = f32[1024,768]{1,0:T(8,128)} fusion(bf16[2,1024,3072]{2,1,0:T(8,128)(2,1)} %all-gather.3.cloned.1.call-done, bf16[768,3072]{1,0:T(8,128)(2,1)} %param.12, bf16[96,8,24,128]{3,2,1,0:T(8,128)(2,1)S(1)} %bitcast.79), kind=kOutput, calls=%fused_computation.15 | convolution fusion | flops 4834197504 | bytes 18874368 | tf_op jit(solution)/shard_map/td,fd->tf/dot_general | solution.py:61
  116.5 0.7 broadcast_in_dim.44
  117.2 0.0 copy-start.1
  117.2 0.0 slice-done
  117.2 0.0 slice-done.1
  117.2 13.3 %fusion.9 = bf16[1024,768]{1,0:T(8,128)(2,1)} fusion(f32[1024,768]{1,0:T(8,128)} %fusion.1, bf16[768,3072]{1,0:T(8,128)(2,1)S(1)} %bitcast.94, bf16[96,8,24,128]{3,2,1,0:T(8,128)(2,1)S(1)} %bitcast.82, bf16[2,1024,3072]{2,1,0:T(8,128)(2,1)} %all-gather.3.cloned.1.call-done), kind=kOutput, calls=%fused_computation.29 | convolution fusion | flops 4849926144 | bytes 20447232 | tf_op jit(solution)/shard_map/td,fd->tf/dot_general | solution.py:68
  130.5 0.0 copy-done
  130.5 0.0 copy-done.1
  130.5 9.7 %multiply_convert_fusion.1 = bf16[768,3072]{1,0:T(8,128)(2,1)} fusion(bf16[1024,768]{1,0:T(8,128)(2,1)} %fusion.9, bf16[2,1024,3072]{2,1,0:T(8,128)(2,1)} %all-gather.3.cloned.1.call-done, bf16[96,8,24,128]{3,2,1,0:T(8,128)(2,1)S(1)} %bitcast.80), kind=kOutput, calls=%fused_computation.10 | convolution fusion | flops 4838916096 | bytes 17301504 | tf_op jit(solution)/shard_map/tf,td->fd/dot_general | solution.py:71
  140.2 5.4 %gather_fusion.1 = bf16[24,32,3072]{2,1,0:T(8,128)(2,1)} fusion(bf16[24,32,3072]{2,1,0:T(8,128)(2,1)} %bitcast.85, s32[1024]{0:T(1024)S(1)} %pad_clamp_fusion.4), kind=kCustom, calls=%fused_computation.1 | custom fusion | bytes 9437280 | tf_op jit(solution)/shard_map/gather | solution.py:57
  145.6 0.0 copy-start.2
  145.6 0.0 reduce-scatter.6.cloned.1.call-update
  145.7 0.0 reduce-scatter.8.cloned.1.call-start
  145.7 0.6 copy-done.2
  146.3 1.6 sort.32
  147.9 11.8 %multiply_convert_fusion = bf16[768,3072]{1,0:T(8,128)(2,1)} fusion(bf16[2,1024,3072]{2,1,0:T(8,128)(2,1)} %all-gather.3.cloned.1.call-done, bf16[96,8,24,128]{3,2,1,0:T(8,128)(2,1)} %bitcast.83, f32[1024,768]{1,0:T(8,128)} %fusion.1), kind=kOutput, calls=%fused_computation.9 | convolution fusion | flops 4845993984 | bytes 18874368 | tf_op jit(solution)/shard_map/tf,td->fd/dot_general | solution.py:65
  159.7 5.5 %gather_fusion.4 = bf16[24,32,3072]{2,1,0:T(8,128)(2,1)} fusion(bf16[24,32,3072]{2,1,0:T(8,128)(2,1)} %bitcast.84, s32[1024]{0:T(1024)S(1)} %pad_clamp_fusion.2), kind=kCustom, calls=%fused_computation.4 | custom fusion | bytes 9437280 | tf_op jit(solution)/shard_map/gather | solution.py:57
  165.2 0.0 reduce-scatter.8.cloned.1.call-update
  165.3 0.0 all-gather.5.cloned.1.call-start
  165.3 0.1 broadcast_in_dim.46
  165.4 0.1 compare_select_fusion.3
  165.5 3.0 gather_fusion.2
  168.5 2.8 broadcast_in_dim.48
  171.3 3.0 gather_fusion
  174.3 0.1 broadcast_in_dim.51
  174.4 3.0 gather_fusion.5
  177.4 2.8 broadcast_in_dim.53
  180.1 3.0 gather_fusion.3
  183.1 18.8 %reduce-scatter.6.cloned.1.call-done = bf16[3,32,3072]{2,1,0:T(8,128)(2,1)} async-done(((bf16[24,32,3072]{2,1,0:T(8,128)(2,1)}), bf16[3,32,3072]{2,1,0:T(8,128)(2,1)}) %reduce-scatter.6.cloned.1.call-update) | async-done | bytes 589840 | tf_op jit(solution)/shard_map/reduce_scatter | solution.py:76
  201.9 59.4 %reduce-scatter.8.cloned.1.call-done = bf16[3,32,3072]{2,1,0:T(8,128)(2,1)} async-done(((bf16[24,32,3072]{2,1,0:T(8,128)(2,1)}), bf16[3,32,3072]{2,1,0:T(8,128)(2,1)}) %reduce-scatter.8.cloned.1.call-update) | async-done | bytes 589840 | tf_op jit(solution)/shard_map/reduce_scatter | solution.py:75
  261.3 4.7 fusion.34
  265.9 0.0 copy-start.3
  265.9 1.1 pad_maximum_fusion.1
  267.0 0.0 all-gather.5.cloned.1.call-update
  267.1 0.0 reduce-scatter.4.cloned.1.call-start
  267.1 0.6 copy-done.3
  267.8 10.7 %convolution_convert_fusion = bf16[1024,3072]{1,0:T(8,128)(2,1)} fusion(bf16[1024,768]{1,0:T(8,128)(2,1)S(1)} %copy-done.3, bf16[768,3072]{1,0:T(8,128)(2,1)} %param.12, bf16[96,8,24,128]{3,2,1,0:T(8,128)(2,1)} %bitcast.81), kind=kOutput, calls=%fused_computation.13 | convolution fusion | flops 4837343232 | bytes 17301504 | tf_op jit(solution)/shard_map/dot_general | solution.py:77
  278.4 0.0 reduce-scatter.4.cloned.1.call-update
  278.5 89.3 %all-gather.5.cloned.1.call-done = bf16[2,24,32,3072]{3,2,1,0:T(8,128)(2,1)} async-done(((bf16[2,3,32,3072]{3,2,1,0:T(8,128)(2,1)}), bf16[2,24,32,3072]{3,2,1,0:T(8,128)(2,1)}) %all-gather.5.cloned.1.call-update) | async-done | bytes 9437200 | tf_op jit(solution)/shard_map/all_gather | solution.py:107
  367.8 9.0 %slice_bitcast_fusion.7 = (bf16[24,32,3072]{2,1,0:T(8,128)(2,1)}, bf16[24,32,3072]{2,1,0:T(8,128)(2,1)}) fusion(bf16[2,24,32,3072]{3,2,1,0:T(8,128)(2,1)} %all-gather.5.cloned.1.call-done), kind=kLoop, calls=%fused_computation.19 | loop fusion | bytes 18874368 | tf_op jit(solution)/shard_map/squeeze | solution.py:108
  376.7 5.5 %gather_fusion.7 = bf16[24,32,3072]{2,1,0:T(8,128)(2,1)} fusion(bf16[24,32,3072]{2,1,0:T(8,128)(2,1)} %get-tuple-element.11, s32[1024]{0:T(1024)S(1)} %pad_clamp_fusion), kind=kCustom, calls=%fused_computation.7 | custom fusion | bytes 9437280 | tf_op jit(solution)/shard_map/gather | solution.py:109
  382.2 5.9 %gather_fusion.6 = bf16[24,32,3072]{2,1,0:T(8,128)(2,1)} fusion(bf16[24,32,3072]{2,1,0:T(8,128)(2,1)} %get-tuple-element.10, s32[1024]{0:T(1024)S(1)} %pad_clamp_fusion.1), kind=kCustom, calls=%fused_computation.6 | custom fusion | bytes 9437280 | tf_op jit(solution)/shard_map/gather | solution.py:108
  388.1 9.1 %pad_maximum_fusion = bf16[2,768,3072]{2,1,0:T(8,128)(2,1)} fusion(bf16[1,768,3072]{2,1,0:T(8,128)(2,1)} %bitcast.77, bf16[1,768,3072]{2,1,0:T(8,128)(2,1)} %bitcast.78), kind=kLoop, calls=%fused_computation.8 | loop fusion | flops 4718592 | bytes 18874368 | tf_op jit(solution)/shard_map/stack | solution.py:110
  397.1 63.7 %reduce-scatter.4.cloned.1.call-done = bf16[64,3072]{1,0:T(8,128)(2,1)} async-done(((bf16[1024,3072]{1,0:T(8,128)(2,1)}), bf16[64,3072]{1,0:T(8,128)(2,1)}) %reduce-scatter.4.cloned.1.call-update) | async-done | bytes 393232 | tf_op jit(solution)/shard_map/reduce_scatter | solution.py:78
  (14 shorter events, 0.1 us)
Async XLA Ops:
  7.2 96.8 %all-gather.3.cloned.1.call-start = ((), (), s32[]{:S(2)}) async-start(), calls=%async_computation.3 | async-start | bytes 13369344 | tf_op jit(solution)/shard_map/all_gather | solution.py:59
  9.3 192.6 %reduce-scatter.6.cloned.1.call-start = ((), (), s32[]{:S(2)}) async-start(), calls=%async_computation.5 | async-start | bytes 5308416 | tf_op jit(solution)/shard_map/reduce_scatter | solution.py:76
  104.0 13.2 %slice-start = ((s8[4718592]{0:T(1024)(128)(4,1)}), s8[4194304]{0:T(1024)(128)(4,1)S(1)}, s32[]{:S(2)}) async-start(s8[4718592]{0:T(1024)(128)(4,1)} %bitcast.93), calls=%async_computation.8 | async-start | bytes 8388608
  104.6 25.9 %copy-start = (bf16[6,128,24,128]{3,2,1,0:T(8,128)(2,1)}, bf16[6,128,24,128]{3,2,1,0:T(8,128)(2,1)S(1)}, u32[]{:S(2)}) copy-start(bf16[6,128,24,128]{3,2,1,0:T(8,128)(2,1)S(1)} %broadcast_in_dim.45) | copy-start | bytes 14155780
  104.6 12.6 %slice-start.1 = ((s8[4718592]{0:T(1024)(128)(4,1)}), s8[524288]{0:T(1024)(128)(4,1)S(1)}, s32[]{:S(2)}) async-start(s8[4718592]{0:T(1024)(128)(4,1)} %bitcast.93), calls=%async_computation.9 | async-start | bytes 1048576
  117.2 13.3 %copy-start.1 = (bf16[6,128,24,128]{3,2,1,0:T(8,128)(2,1)}, bf16[6,128,24,128]{3,2,1,0:T(8,128)(2,1)S(1)}, u32[]{:S(2)}) copy-start(bf16[6,128,24,128]{3,2,1,0:T(8,128)(2,1)S(1)} %broadcast_in_dim.44) | copy-start | bytes 14155780
  145.6 0.7 copy-start.2
  145.7 115.6 %reduce-scatter.8.cloned.1.call-start = ((), (), s32[]{:S(2)}) async-start(), calls=%async_computation.6 | async-start | bytes 5308416 | tf_op jit(solution)/shard_map/reduce_scatter | solution.py:75
  165.3 202.5 %all-gather.5.cloned.1.call-start = ((), (), s32[]{:S(2)}) async-start(), calls=%async_computation.7 | async-start | bytes 10616832 | tf_op jit(solution)/shard_map/all_gather | solution.py:107
  265.9 1.8 copy-start.3
  267.1 193.8 %reduce-scatter.4.cloned.1.call-start = ((), (), s32[]{:S(2)}) async-start(), calls=%async_computation.4 | async-start | bytes 6684672 | tf_op jit(solution)/shard_map/reduce_scatter | solution.py:78
Sparse Core Ops, SparseCore 0:
  11.0 92.8 all-gather.2
  145.8 56.0 reduce-scatter.5
  204.3 56.9 reduce-scatter.7
  267.2 100.5 all-gather.4
  372.4 88.4 reduce-scatter.3

commit v4 on v3

--- a/solution.py
+++ b/solution.py
@@ -46,8 +46,6 @@
     bucket_rows = hidden_local // buckets
     keep_up = expand_mask(mask_up)
     keep_down = expand_mask(mask_down)
-    up_live = w_up * keep_up
-    down_live = w_down * keep_down
     place_up = slot_places(order_up, owners, owned)
     place_down = slot_places(order_down, owners, owned)
     sorter_up = jnp.argsort(place_up)
@@ -56,22 +54,31 @@
     def owner_order(matrix, sorter):
         return matrix.reshape(buckets, bucket_rows, width)[sorter]
 
+    def down_layout(matrix):
+        return owner_order(matrix, sorter_down).reshape(hidden_local, width)
+
+    keep_up_s = down_layout(keep_up)
+    keep_down_s = down_layout(keep_down)
+    up_live = down_layout(w_up) * keep_up_s
+    down_live = down_layout(w_down) * keep_down_s
+    up_from_down = jnp.argsort(sorter_down)[sorter_up]
+
     both_rows = lax.all_gather(jnp.stack([tokens_in, out_grad]), "mp", axis=1, tiled=True)
     feat_rows, grad_rows = both_rows[0], both_rows[1]
     hidden_pre = jnp.einsum("td,fd->tf", feat_rows, up_live, preferred_element_type=jnp.float32)
     activation, gelu_back = jax.vjp(jax.nn.gelu, hidden_pre)
     act_low = activation.astype(jnp.bfloat16)
     grad_down = (
-        jnp.einsum("tf,td->fd", act_low, grad_rows, preferred_element_type=jnp.float32) * keep_down
+        jnp.einsum("tf,td->fd", act_low, grad_rows, preferred_element_type=jnp.float32) * keep_down_s
     ).astype(jnp.bfloat16)
-    down_sorted = owner_order(grad_down, sorter_down)
+    down_sorted = grad_down.reshape(buckets, bucket_rows, width)
     act_grad = jnp.einsum("td,fd->tf", grad_rows, down_live, preferred_element_type=jnp.float32)
     hidden_grad = gelu_back(act_grad)[0].astype(jnp.bfloat16)
     grad_up = (
         jnp.einsum("tf,td->fd", hidden_grad, feat_rows, preferred_element_type=jnp.float32)
-        * keep_up
+        * keep_up_s
     ).astype(jnp.bfloat16)
-    up_sorted = owner_order(grad_up, sorter_up)
+    up_sorted = owner_order(grad_up, up_from_down)
     down_summed = lax.psum_scatter(down_sorted, "dp", scatter_dimension=0, tiled=True).astype(jnp.float32)
     up_summed = lax.psum_scatter(up_sorted, "dp", scatter_dimension=0, tiled=True).astype(jnp.float32)
     partial_term = jnp.dot(hidden_grad, up_live, preferred_element_type=jnp.float32)

time: 468 us -> 442 us (0.944)
  waiting for transfers between devices: 322 us -> 274 us
  other arithmetic: 22.3 us -> 39.7 us
  local copies, waits for them, and re-layouts: 51.4 us -> 67 us
  matrix products: 57.3 us -> 46.4 us
    reduce_scatter x1, waiting for transfers between devices: 59.4 us -> 0.02 us  [layer(): lax.psum_scatter(down_sorted, 'dp', scatter_dimension=0, tiled=True)]
    reduce_scatter x1, waiting for transfers between devices: 18.8 us -> 58.9 us  [layer(): lax.psum_scatter(up_sorted, 'dp', scatter_dimension=0, tiled=True)]
    all_gather x1, waiting for transfers between devices: 90.9 us -> 60.1 us  [layer(): lax.all_gather(jnp.stack([tokens_in, out_grad]), 'mp', axis=1, tiled=True)]
    gather x2 -> x5, local copies, waits for them, and re-layouts: 10.9 us -> 27.8 us  [owner_order(): return matrix.reshape(buckets, bucket_rows, width)[sorter]]
    mul x0 -> x2, other arithmetic: none -> 16.4 us  [the longest x1 8.27 us: layer(): up_live = down_layout(w_up) * keep_up_s]
  transfers between devices with their start and end apart: 5 -> 5, of which waited for: 5 -> 4; matrix products, arithmetic and copies ran while one was open for 17% -> 29% of each run, Pallas kernels for 0% -> 0%
where the time goes in v4:
time: 442 us; the launch traced here: 441 us
  waiting for transfers between devices  274 us (62%)
  local copies, waits for them, and re-layouts  67 us (15%)
  matrix products  46.4 us (10%)
  other arithmetic  39.7 us (9%)
  between operations  14 us (3%)
    all_gather x1, waiting for transfers between devices, layer(): all_steps = lax.all_gather(stacked, 'dp', axis=1, tiled=True)  90.7 us
    reduce_scatter x1, waiting for transfers between devices, layer(): lax.psum_scatter(lax.optimization_barrier(partial_term.astype(jnp.bfloat1...  63.7 us
    all_gather x1, waiting for transfers between devices, layer(): lax.all_gather(jnp.stack([tokens_in, out_grad]), 'mp', axis=1, tiled=True)  60.1 us
    reduce_scatter x1, waiting for transfers between devices, layer(): lax.psum_scatter(up_sorted, 'dp', scatter_dimension=0, tiled=True)  58.9 us
    gather x5, local copies, waits for them, and re-layouts, owner_order(): return matrix.reshape(buckets, bucket_rows, width)[sorter]  27.8 us
    gather x4, local copies, waits for them, and re-layouts, owned_rows(): matrix.reshape(buckets, bucket_rows, width)[chosen].astype(jnp.float32)  11.9 us
    dot_general x1, matrix products, layer(): jnp.einsum('td,fd->tf', grad_rows, down_live, preferred_element_type=jnp....  10.9 us
    dot_general x1, matrix products, layer(): jnp.einsum('tf,td->fd', hidden_grad, feat_rows, preferred_element_type=jn...  10.2 us
  transfers between devices with their start and end apart: 5, of which 4 were waited for; matrix products, arithmetic and copies ran while one was open for 29% of the time, Pallas kernels for 0%

profile of v4, /device:TPU:0, one launch (start us, length us, event | category | flops | bytes accessed | tf_op | source)
XLA Modules:
  0.0 441.4 jit_solution(18223520384393789640)
XLA Ops:
  7.2 0.0 copy-start.1
  7.2 0.0 all-gather.3.cloned.1.call-start
  7.2 2.1 pad_maximum_fusion.2
  9.3 0.0 all-gather.3.cloned.1.call-update
  9.3 0.0 reduce-scatter.8.cloned.1.call-start
  9.4 0.7 convert_element_type.60
  10.1 0.7 convert_element_type.59
  10.8 0.1 broadcast_in_dim.45
  10.9 0.1 broadcast_in_dim.48
  11.0 0.0 copy-done.1
  11.1 1.6 sort.45
  12.7 2.7 broadcast_in_dim.50
  15.4 5.6 %gather_fusion.3 = bf16[24,32,3072]{2,1,0:T(8,128)(2,1)} fusion(bf16[24,32,3072]{2,1,0:T(8,128)(2,1)} %broadcast_in_dim.50, s32[1024]{0:T(1024)S(1)} %pad_clamp_fusion.6), kind=kCustom, calls=%fused_computation.3 | custom fusion | bytes 9437280 | tf_op jit(solution)/shard_map/gather | solution.py:55
  20.9 2.7 broadcast_in_dim.47
  23.7 5.7 %gather_fusion.1 = bf16[24,32,3072]{2,1,0:T(8,128)(2,1)} fusion(bf16[24,32,3072]{2,1,0:T(8,128)(2,1)} %broadcast_in_dim.47, s32[1024]{0:T(1024)S(1)} %pad_clamp_fusion.6), kind=kCustom, calls=%fused_computation.1 | custom fusion | bytes 9437280 | tf_op jit(solution)/shard_map/gather | solution.py:55
  29.4 5.6 %gather_fusion.2 = bf16[24,32,3072]{2,1,0:T(8,128)(2,1)} fusion(bf16[24,32,3072]{2,1,0:T(8,128)(2,1)} %bitcast.83, s32[1024]{0:T(1024)S(1)} %pad_clamp_fusion.6), kind=kCustom, calls=%fused_computation.2 | custom fusion | bytes 9437280 | tf_op jit(solution)/shard_map/gather | solution.py:55
  34.9 0.0 slice-start.2
  34.9 8.3 %mul.144 = bf16[24,32,3072]{2,1,0:T(8,128)(2,1)} multiply(bf16[24,32,3072]{2,1,0:T(8,128)(2,1)} %gather_fusion.2, bf16[24,32,3072]{2,1,0:T(8,128)(2,1)} %gather_fusion.3) | non-fusion elementwise | flops 2359296 | bytes 14155776 | tf_op jit(solution)/shard_map/mul | solution.py:62
  43.2 60.1 %all-gather.3.cloned.1.call-done = bf16[2,1024,3072]{2,1,0:T(8,128)(2,1)} async-done(((bf16[2,64,3072]{2,1,0:T(8,128)(2,1)}), bf16[2,1024,3072]{2,1,0:T(8,128)(2,1)}) %all-gather.3.cloned.1.call-update) | async-done | bytes 12582928 | tf_op jit(solution)/shard_map/all_gather | solution.py:66
  103.3 8.7 %fusion.3 = f32[1024,768]{1,0:T(8,128)S(1)} fusion(bf16[768,3072]{1,0:T(8,128)(2,1)} %bitcast.87, bf16[2,1024,3072]{2,1,0:T(8,128)(2,1)} %all-gather.3.cloned.1.call-done), kind=kOutput, calls=%fused_computation.21 | convolution fusion | flops 4831838208 | bytes 14155776 | tf_op jit(solution)/shard_map/td,fd->tf/dot_general | solution.py:68
  112.1 0.0 copy-start.5
  112.1 0.0 slice-done.2
  112.1 0.0 slice-done.3
  112.1 0.3 copy-done
  112.4 7.4 %fusion = bf16[768,3072]{1,0:T(8,128)(2,1)} fusion(bf16[768,3072]{1,0:T(8,128)(2,1)S(1)} %bitcast.80, bf16[2,1024,3072]{2,1,0:T(8,128)(2,1)S(1)} %copy-done, f32[1024,768]{1,0:T(8,128)S(1)} %fusion.3), kind=kOutput, calls=%fused_computation.14 | convolution fusion | flops 4845993984 | bytes 18874368 | tf_op jit(solution)/shard_map/tf,td->fd/dot_general | solution.py:72
  119.7 0.0 copy-done.5
  119.7 0.0 reduce-scatter.8.cloned.1.call-update
  119.8 0.2 reduce-scatter.6.cloned.1.call-start
  120.0 1.6 sort.47
  121.6 5.5 %gather_fusion = bf16[24,32,3072]{2,1,0:T(8,128)(2,1)} fusion(bf16[24,32,3072]{2,1,0:T(8,128)(2,1)} %bitcast.85, s32[1024]{0:T(1024)S(1)} %pad_clamp_fusion.6), kind=kCustom, calls=%fused_computation | custom fusion | bytes 9437280 | tf_op jit(solution)/shard_map/gather | solution.py:55
  127.1 8.1 %mul.142 = bf16[24,32,3072]{2,1,0:T(8,128)(2,1)} multiply(bf16[24,32,3072]{2,1,0:T(8,128)(2,1)} %gather_fusion, bf16[24,32,3072]{2,1,0:T(8,128)(2,1)} %gather_fusion.1) | non-fusion elementwise | flops 2359296 | bytes 14155776 | tf_op jit(solution)/shard_map/mul | solution.py:63
  135.2 0.0 copy-done.2
  135.3 1.6 sort.46
  136.9 0.7 gather_fusion.5
  137.6 0.0 slice-start.1
  137.6 10.9 %fusion.10 = bf16[1024,768]{1,0:T(8,128)(2,1)S(1)} fusion(f32[1024,768]{1,0:T(8,128)} %copy-done.5, bf16[768,3072]{1,0:T(8,128)(2,1)} %bitcast.89, bf16[2,1024,3072]{2,1,0:T(8,128)(2,1)} %all-gather.3.cloned.1.call-done), kind=kOutput, calls=%fused_computation.32 | convolution fusion | flops 4847566848 | bytes 15728640 | tf_op jit(solution)/shard_map/td,fd->tf/dot_general | solution.py:75
  148.5 0.0 copy-start.3
  148.5 0.0 slice-done
  148.5 0.0 slice-done.1
  148.5 10.2 %fusion.1 = bf16[768,3072]{1,0:T(8,128)(2,1)} fusion(bf16[768,3072]{1,0:T(8,128)(2,1)S(1)} %bitcast.77, bf16[1024,768]{1,0:T(8,128)(2,1)S(1)} %fusion.10, bf16[2,1024,3072]{2,1,0:T(8,128)(2,1)} %all-gather.3.cloned.1.call-done), kind=kOutput, calls=%fused_computation.16 | convolution fusion | flops 4838916096 | bytes 17301504 | tf_op jit(solution)/shard_map/tf,td->fd/dot_general | solution.py:78
  158.7 0.0 copy-done.3
  158.7 5.5 %gather_fusion.6 = bf16[24,32,3072]{2,1,0:T(8,128)(2,1)} fusion(bf16[24,32,3072]{2,1,0:T(8,128)(2,1)} %bitcast.91, s32[1024]{0:T(1024)S(1)} %pad_clamp_fusion.3), kind=kCustom, calls=%fused_computation.6 | custom fusion | bytes 9437280 | tf_op jit(solution)/shard_map/gather | solution.py:55
  164.2 0.0 reduce-scatter.6.cloned.1.call-update
  164.3 0.0 all-gather.5.cloned.1.call-start
  164.3 0.1 compare_select_fusion.2
  164.4 3.0 gather_fusion.7
  167.4 3.0 gather_fusion.4
  170.4 3.0 gather_fusion.9
  173.4 3.0 gather_fusion.8
  176.4 0.0 reduce-scatter.8.cloned.1.call-done
  176.4 58.9 %reduce-scatter.6.cloned.1.call-done = bf16[3,32,3072]{2,1,0:T(8,128)(2,1)} async-done(((bf16[24,32,3072]{2,1,0:T(8,128)(2,1)}), bf16[3,32,3072]{2,1,0:T(8,128)(2,1)}) %reduce-scatter.6.cloned.1.call-update) | async-done | bytes 589840 | tf_op jit(solution)/shard_map/reduce_scatter | solution.py:83
  235.3 4.7 %fusion.35 = (bf16[1,3,32,3072]{3,2,1,0:T(8,128)(2,1)S(1)}, bf16[1,3,32,3072]{3,2,1,0:T(8,128)(2,1)S(1)}) fusion(bf16[3,32,3072]{2,1,0:T(8,128)(2,1)S(1)} %gather_fusion.7, f32[2,1,3,32,3072]{4,3,2,1,0:T(8,128)} %param.19, bf16[3,32,3072]{2,1,0:T(8,128)(2,1)} %reduce-scatter.6.cloned.1.call-done, f32[2,1,3,32,3072]{4,3,2,1,0:T(8,128)} %param.18, ...), kind=kLoop, calls=%fused_computation.64 | loop fusion | flops 10616832 | bytes 9437184 | tf_op jit(solution)/shard_map/stack | solution.py:113
  240.0 1.1 pad_maximum_fusion.1
  241.1 0.0 all-gather.5.cloned.1.call-update
  241.1 0.3 reduce-scatter.4.cloned.1.call-start
  241.4 0.4 copy-done.4
  241.8 9.2 %convolution_convert_fusion = bf16[1024,3072]{1,0:T(8,128)(2,1)} fusion(bf16[1024,768]{1,0:T(8,128)(2,1)S(1)} %copy-done.4, bf16[768,3072]{1,0:T(8,128)(2,1)} %bitcast.88), kind=kOutput, calls=%fused_computation.19 | convolution fusion | flops 4834983936 | bytes 12582912 | tf_op jit(solution)/shard_map/dot_general | solution.py:84
  251.1 0.0 reduce-scatter.4.cloned.1.call-update
  251.1 90.7 %all-gather.5.cloned.1.call-done = bf16[2,24,32,3072]{3,2,1,0:T(8,128)(2,1)} async-done(((bf16[2,3,32,3072]{3,2,1,0:T(8,128)(2,1)}), bf16[2,24,32,3072]{3,2,1,0:T(8,128)(2,1)}) %all-gather.5.cloned.1.call-update) | async-done | bytes 9437200 | tf_op jit(solution)/shard_map/all_gather | solution.py:114
  341.9 8.9 %slice_bitcast_fusion.7 = (bf16[24,32,3072]{2,1,0:T(8,128)(2,1)}, bf16[24,32,3072]{2,1,0:T(8,128)(2,1)}) fusion(bf16[2,24,32,3072]{3,2,1,0:T(8,128)(2,1)} %all-gather.5.cloned.1.call-done), kind=kLoop, calls=%fused_computation.23 | loop fusion | bytes 18874368 | tf_op jit(solution)/shard_map/squeeze | solution.py:115
  350.8 5.5 %gather_fusion.10 = bf16[24,32,3072]{2,1,0:T(8,128)(2,1)} fusion(bf16[24,32,3072]{2,1,0:T(8,128)(2,1)} %get-tuple-element.12, s32[1024]{0:T(1024)S(1)} %pad_clamp_fusion.1), kind=kCustom, calls=%fused_computation.10 | custom fusion | bytes 9437280 | tf_op jit(solution)/shard_map/gather | solution.py:115
  356.3 5.8 %gather_fusion.11 = bf16[24,32,3072]{2,1,0:T(8,128)(2,1)} fusion(bf16[24,32,3072]{2,1,0:T(8,128)(2,1)} %get-tuple-element.13, s32[1024]{0:T(1024)S(1)} %pad_clamp_fusion), kind=kCustom, calls=%fused_computation.11 | custom fusion | bytes 9437280 | tf_op jit(solution)/shard_map/gather | solution.py:116
  362.1 9.1 %pad_maximum_fusion = bf16[2,768,3072]{2,1,0:T(8,128)(2,1)} fusion(bf16[1,768,3072]{2,1,0:T(8,128)(2,1)} %bitcast.82, bf16[1,768,3072]{2,1,0:T(8,128)(2,1)} %bitcast.81), kind=kLoop, calls=%fused_computation.12 | loop fusion | flops 4718592 | bytes 18874368 | tf_op jit(solution)/shard_map/stack | solution.py:117
  371.2 63.7 %reduce-scatter.4.cloned.1.call-done = bf16[64,3072]{1,0:T(8,128)(2,1)} async-done(((bf16[1024,3072]{1,0:T(8,128)(2,1)}), bf16[64,3072]{1,0:T(8,128)(2,1)}) %reduce-scatter.4.cloned.1.call-update) | async-done | bytes 393232 | tf_op jit(solution)/shard_map/reduce_scatter | solution.py:85
  (24 shorter events, 0.2 us)
Async XLA Ops:
  7.2 3.9 copy-start.1
  7.2 96.2 %all-gather.3.cloned.1.call-start = ((), (), s32[]{:S(2)}) async-start(), calls=%async_computation.3 | async-start | bytes 13369344 | tf_op jit(solution)/shard_map/all_gather | solution.py:66
  9.3 167.0 %reduce-scatter.8.cloned.1.call-start = ((), (), s32[]{:S(2)}) async-start(), calls=%async_computation.6 | async-start | bytes 5308416 | tf_op jit(solution)/shard_map/reduce_scatter | solution.py:82
  34.9 77.2 %slice-start.2 = ((s8[4718592]{0:T(1024)(128)(4,1)}), s8[524288]{0:T(1024)(128)(4,1)S(1)}, s32[]{:S(2)}) async-start(s8[4718592]{0:T(1024)(128)(4,1)} %bitcast.78), calls=%async_computation.10 | async-start | bytes 1048576
  103.3 8.8 %slice-start.3 = ((s8[4718592]{0:T(1024)(128)(4,1)}), s8[4194304]{0:T(1024)(128)(4,1)S(1)}, s32[]{:S(2)}) async-start(s8[4718592]{0:T(1024)(128)(4,1)} %bitcast.78), calls=%async_computation.11 | async-start | bytes 8388608
  103.3 9.0 %copy-start = (bf16[2,1024,3072]{2,1,0:T(8,128)(2,1)S(1)}, bf16[2,1024,3072]{2,1,0:T(8,128)(2,1)}, u32[]{:S(2)}) copy-start(bf16[2,1024,3072]{2,1,0:T(8,128)(2,1)} %all-gather.3.cloned.1.call-done) | copy-start | bytes 37748740
  112.1 7.7 %copy-start.5 = (f32[1024,768]{1,0:T(8,128)}, f32[1024,768]{1,0:T(8,128)S(1)}, u32[]{:S(2)}) copy-start(f32[1024,768]{1,0:T(8,128)S(1)} %fusion.3) | copy-start | bytes 9437188
  119.8 115.6 %reduce-scatter.6.cloned.1.call-start = ((), (), s32[]{:S(2)}) async-start(), calls=%async_computation.5 | async-start | bytes 5308416 | tf_op jit(solution)/shard_map/reduce_scatter | solution.py:83
  127.1 8.1 %copy-start.2 = (s32[24]{0:T(128)S(1)}, s32[24]{0:T(128)}, u32[]{:S(2)}) copy-start(s32[24]{0:T(128)} %param.16) | copy-start | bytes 292
  127.1 21.4 %slice-start = ((s8[4718592]{0:T(1024)(128)(4,1)}), s8[524288]{0:T(1024)(128)(4,1)S(1)}, s32[]{:S(2)}) async-start(s8[4718592]{0:T(1024)(128)(4,1)} %bitcast.75), calls=%async_computation.8 | async-start | bytes 1048576
  137.6 10.9 %slice-start.1 = ((s8[4718592]{0:T(1024)(128)(4,1)}), s8[4194304]{0:T(1024)(128)(4,1)S(1)}, s32[]{:S(2)}) async-start(s8[4718592]{0:T(1024)(128)(4,1)} %bitcast.75), calls=%async_computation.9 | async-start | bytes 8388608
  148.5 10.3 %copy-start.3 = (bf16[1024,768]{1,0:T(8,128)(2,1)}, bf16[1024,768]{1,0:T(8,128)(2,1)S(1)}, u32[]{:S(2)}) copy-start(bf16[1024,768]{1,0:T(8,128)(2,1)S(1)} %fusion.10) | copy-start | bytes 4718596
  164.3 177.6 %all-gather.5.cloned.1.call-start = ((), (), s32[]{:S(2)}) async-start(), calls=%async_computation.7 | async-start | bytes 10616832 | tf_op jit(solution)/shard_map/all_gather | solution.py:114
  240.0 1.8 copy-start.4
  241.1 193.8 %reduce-scatter.4.cloned.1.call-start = ((), (), s32[]{:S(2)}) async-start(), calls=%async_computation.4 | async-start | bytes 6684672 | tf_op jit(solution)/shard_map/reduce_scatter | solution.py:85
Sparse Core Ops, SparseCore 0:
  10.5 92.8 all-gather.2
  119.9 56.0 reduce-scatter.7
  178.4 56.9 reduce-scatter.5
  241.3 100.5 all-gather.4
  346.5 88.3 reduce-scatter.3

commit v5 on v4

--- a/solution.py
+++ b/solution.py
@@ -40,6 +40,7 @@
     moment_two,
 ):
     owners = lax.axis_size("dp")
+    local_rows = tokens_in.shape[0]
     hidden_local, width = w_up.shape
     buckets = order_up.shape[0]
     owned = buckets // owners
@@ -82,14 +83,11 @@
     down_summed = lax.psum_scatter(down_sorted, "dp", scatter_dimension=0, tiled=True).astype(jnp.float32)
     up_summed = lax.psum_scatter(up_sorted, "dp", scatter_dimension=0, tiled=True).astype(jnp.float32)
     partial_term = jnp.dot(hidden_grad, up_live, preferred_element_type=jnp.float32)
-    input_grad = lax.psum_scatter(
-        lax.optimization_barrier(partial_term.astype(jnp.bfloat16))
-        .astype(jnp.float32)
-        .astype(jnp.bfloat16),
-        "mp",
-        scatter_dimension=0,
-        tiled=True,
+    shards_mp = lax.axis_size("mp")
+    shares = lax.all_to_all(
+        partial_term.astype(jnp.bfloat16).reshape(shards_mp, local_rows, width), "mp", 0, 0, tiled=True
     )
+    input_grad = shares.astype(jnp.float32).sum(axis=0).astype(jnp.bfloat16)
     owner_index = lax.axis_index("dp")
 
     def owned_rows(matrix, sorter):

time: 442 us -> 446 us (level)
  waiting for transfers between devices: 274 us -> 266 us
  starting transfers between devices: 0.61 us -> 7.13 us
    all_to_all x0 -> x1, waiting for transfers between devices: none -> 142 us  [layer(): lax.all_to_all(partial_term.astype(jnp.bfloat16).reshape(shards_mp, local...]
    all_gather x1, waiting for transfers between devices: 90.7 us -> 4.84 us  [layer(): all_steps = lax.all_gather(stacked, 'dp', axis=1, tiled=True)]
    reduce_scatter x1 -> x0, waiting for transfers between devices: 63.7 us -> none  [layer(): lax.psum_scatter(lax.optimization_barrier(partial_term.astype(jnp.bfloat1...]
    all_to_all x0 -> x1, starting transfers between devices: none -> 6.56 us  [layer(): lax.all_to_all(partial_term.astype(jnp.bfloat16).reshape(shards_mp, local...]
    reduce_sum x0 -> x1, other arithmetic: none -> 4.79 us  [layer(): input_grad = shares.astype(jnp.float32).sum(axis=0).astype(jnp.bfloat16)]
  transfers between devices with their start and end apart: 5 -> 5, of which waited for: 4 -> 4; matrix products, arithmetic and copies ran while one was open for 29% -> 23% of each run, Pallas kernels for 0% -> 0%
where the time goes in v5:
time: 446 us; the launch traced here: 444 us
  waiting for transfers between devices  266 us (60%)
  local copies, waits for them, and re-layouts  67.3 us (15%)
  matrix products  46.3 us (10%)
  other arithmetic  43.8 us (10%)
  between operations  14 us (3%)
  starting transfers between devices  7.13 us (2%)
    all_to_all x1, waiting for transfers between devices, layer(): lax.all_to_all(partial_term.astype(jnp.bfloat16).reshape(shards_mp, local...  142 us
    all_gather x1, waiting for transfers between devices, layer(): lax.all_gather(jnp.stack([tokens_in, out_grad]), 'mp', axis=1, tiled=True)  60.2 us
    reduce_scatter x1, waiting for transfers between devices, layer(): lax.psum_scatter(up_sorted, 'dp', scatter_dimension=0, tiled=True)  58.6 us
    gather x5, local copies, waits for them, and re-layouts, owner_order(): return matrix.reshape(buckets, bucket_rows, width)[sorter]  28 us
    gather x4, local copies, waits for them, and re-layouts, owned_rows(): matrix.reshape(buckets, bucket_rows, width)[chosen].astype(jnp.float32)  11.9 us
    dot_general x1, matrix products, layer(): jnp.einsum('td,fd->tf', grad_rows, down_live, preferred_element_type=jnp....  10.8 us
    dot_general x1, matrix products, layer(): jnp.einsum('tf,td->fd', hidden_grad, feat_rows, preferred_element_type=jn...  10.2 us
    dot_general x1, matrix products, layer(): jnp.dot(hidden_grad, up_live, preferred_element_type=jnp.float32)  9.24 us
  transfers between devices with their start and end apart: 5, of which 4 were waited for; matrix products, arithmetic and copies ran while one was open for 23% of the time, Pallas kernels for 0%

profile of v5, /device:TPU:0, one launch (start us, length us, event | category | flops | bytes accessed | tf_op | source)
XLA Modules:
  0.0 444.3 jit_solution(10944031827188391875)
XLA Ops:
  7.2 0.0 copy-start.1
  7.2 0.0 all-gather.3.cloned.1.call-start
  7.2 2.1 pad_maximum_fusion.2
  9.3 0.0 all-gather.3.cloned.1.call-update
  9.3 0.0 reduce-scatter.5.cloned.1.call-start
  9.4 0.7 convert_element_type.60
  10.1 0.7 convert_element_type.59
  10.8 0.1 broadcast_in_dim.45
  10.9 0.1 broadcast_in_dim.48
  11.0 0.0 copy-done.1
  11.1 1.6 sort.45
  12.7 2.7 broadcast_in_dim.50
  15.4 5.6 %gather_fusion.3 = bf16[24,32,3072]{2,1,0:T(8,128)(2,1)} fusion(bf16[24,32,3072]{2,1,0:T(8,128)(2,1)} %broadcast_in_dim.50, s32[1024]{0:T(1024)S(1)} %pad_clamp_fusion.6), kind=kCustom, calls=%fused_computation.3 | custom fusion | bytes 9437280 | tf_op jit(solution)/shard_map/gather | solution.py:56
  21.0 2.8 broadcast_in_dim.47
  23.7 5.7 %gather_fusion.1 = bf16[24,32,3072]{2,1,0:T(8,128)(2,1)} fusion(bf16[24,32,3072]{2,1,0:T(8,128)(2,1)} %broadcast_in_dim.47, s32[1024]{0:T(1024)S(1)} %pad_clamp_fusion.6), kind=kCustom, calls=%fused_computation.1 | custom fusion | bytes 9437280 | tf_op jit(solution)/shard_map/gather | solution.py:56
  29.5 5.6 %gather_fusion.2 = bf16[24,32,3072]{2,1,0:T(8,128)(2,1)} fusion(bf16[24,32,3072]{2,1,0:T(8,128)(2,1)} %bitcast.85, s32[1024]{0:T(1024)S(1)} %pad_clamp_fusion.6), kind=kCustom, calls=%fused_computation.2 | custom fusion | bytes 9437280 | tf_op jit(solution)/shard_map/gather | solution.py:56
  35.0 0.0 slice-start.2
  35.0 8.2 %mul.144 = bf16[24,32,3072]{2,1,0:T(8,128)(2,1)} multiply(bf16[24,32,3072]{2,1,0:T(8,128)(2,1)} %gather_fusion.2, bf16[24,32,3072]{2,1,0:T(8,128)(2,1)} %gather_fusion.3) | non-fusion elementwise | flops 2359296 | bytes 14155776 | tf_op jit(solution)/shard_map/mul | solution.py:63
  43.2 60.2 %all-gather.3.cloned.1.call-done = bf16[2,1024,3072]{2,1,0:T(8,128)(2,1)} async-done(((bf16[2,64,3072]{2,1,0:T(8,128)(2,1)}), bf16[2,1024,3072]{2,1,0:T(8,128)(2,1)}) %all-gather.3.cloned.1.call-update) | async-done | bytes 12582928 | tf_op jit(solution)/shard_map/all_gather | solution.py:67
  103.4 8.7 %fusion.3 = f32[1024,768]{1,0:T(8,128)S(1)} fusion(bf16[768,3072]{1,0:T(8,128)(2,1)} %bitcast.89, bf16[2,1024,3072]{2,1,0:T(8,128)(2,1)} %all-gather.3.cloned.1.call-done), kind=kOutput, calls=%fused_computation.21 | convolution fusion | flops 4831838208 | bytes 14155776 | tf_op jit(solution)/shard_map/td,fd->tf/dot_general | solution.py:69
  112.1 0.0 copy-start.5
  112.1 0.0 slice-done.2
  112.2 0.0 slice-done.3
  112.2 0.3 copy-done
  112.4 7.3 %fusion = bf16[768,3072]{1,0:T(8,128)(2,1)} fusion(bf16[768,3072]{1,0:T(8,128)(2,1)S(1)} %bitcast.81, bf16[2,1024,3072]{2,1,0:T(8,128)(2,1)S(1)} %copy-done, f32[1024,768]{1,0:T(8,128)S(1)} %fusion.3), kind=kOutput, calls=%fused_computation.14 | convolution fusion | flops 4845993984 | bytes 18874368 | tf_op jit(solution)/shard_map/tf,td->fd/dot_general | solution.py:73
  119.8 0.0 copy-done.5
  119.8 0.0 reduce-scatter.5.cloned.1.call-update
  119.8 0.2 reduce-scatter.3.cloned.1.call-start
  120.0 1.6 sort.47
  121.6 5.5 %gather_fusion = bf16[24,32,3072]{2,1,0:T(8,128)(2,1)} fusion(bf16[24,32,3072]{2,1,0:T(8,128)(2,1)} %bitcast.87, s32[1024]{0:T(1024)S(1)} %pad_clamp_fusion.6), kind=kCustom, calls=%fused_computation | custom fusion | bytes 9437280 | tf_op jit(solution)/shard_map/gather | solution.py:56
  127.2 8.2 %mul.142 = bf16[24,32,3072]{2,1,0:T(8,128)(2,1)} multiply(bf16[24,32,3072]{2,1,0:T(8,128)(2,1)} %gather_fusion, bf16[24,32,3072]{2,1,0:T(8,128)(2,1)} %gather_fusion.1) | non-fusion elementwise | flops 2359296 | bytes 14155776 | tf_op jit(solution)/shard_map/mul | solution.py:64
  135.3 0.0 copy-done.2
  135.4 1.6 sort.46
  137.0 0.7 gather_fusion.5
  137.7 0.0 slice-start.1
  137.7 10.8 %fusion.10 = bf16[1024,768]{1,0:T(8,128)(2,1)S(1)} fusion(f32[1024,768]{1,0:T(8,128)} %copy-done.5, bf16[768,3072]{1,0:T(8,128)(2,1)} %bitcast.91, bf16[2,1024,3072]{2,1,0:T(8,128)(2,1)} %all-gather.3.cloned.1.call-done), kind=kOutput, calls=%fused_computation.32 | convolution fusion | flops 4847566848 | bytes 15728640 | tf_op jit(solution)/shard_map/td,fd->tf/dot_general | solution.py:76
  148.6 0.0 copy-start.3
  148.6 0.0 slice-done
  148.6 0.0 slice-done.1
  148.6 10.2 %fusion.1 = bf16[768,3072]{1,0:T(8,128)(2,1)} fusion(bf16[768,3072]{1,0:T(8,128)(2,1)S(1)} %bitcast.78, bf16[1024,768]{1,0:T(8,128)(2,1)S(1)} %fusion.10, bf16[2,1024,3072]{2,1,0:T(8,128)(2,1)} %all-gather.3.cloned.1.call-done), kind=kOutput, calls=%fused_computation.16 | convolution fusion | flops 4838916096 | bytes 17301504 | tf_op jit(solution)/shard_map/tf,td->fd/dot_general | solution.py:79
  158.8 0.0 copy-done.3
  158.8 5.6 %gather_fusion.6 = bf16[24,32,3072]{2,1,0:T(8,128)(2,1)} fusion(bf16[24,32,3072]{2,1,0:T(8,128)(2,1)} %bitcast.93, s32[1024]{0:T(1024)S(1)} %pad_clamp_fusion.3), kind=kCustom, calls=%fused_computation.6 | custom fusion | bytes 9437280 | tf_op jit(solution)/shard_map/gather | solution.py:56
  164.4 0.0 reduce-scatter.3.cloned.1.call-update
  164.5 0.3 all-gather.5.cloned.1.call-start
  164.7 0.1 compare_select_fusion.2
  164.8 3.0 gather_fusion.7
  167.8 3.0 gather_fusion.4
  170.8 3.0 gather_fusion.9
  173.8 3.0 gather_fusion.8
  176.8 0.0 reduce-scatter.5.cloned.1.call-done
  176.8 58.6 %reduce-scatter.3.cloned.1.call-done = bf16[3,32,3072]{2,1,0:T(8,128)(2,1)} async-done(((bf16[24,32,3072]{2,1,0:T(8,128)(2,1)}), bf16[3,32,3072]{2,1,0:T(8,128)(2,1)}) %reduce-scatter.3.cloned.1.call-update) | async-done | bytes 589840 | tf_op jit(solution)/shard_map/reduce_scatter | solution.py:84
  235.4 4.7 %fusion.35 = (bf16[1,3,32,3072]{3,2,1,0:T(8,128)(2,1)S(1)}, bf16[1,3,32,3072]{3,2,1,0:T(8,128)(2,1)S(1)}) fusion(bf16[3,32,3072]{2,1,0:T(8,128)(2,1)S(1)} %gather_fusion.7, f32[2,1,3,32,3072]{4,3,2,1,0:T(8,128)} %param.19, bf16[3,32,3072]{2,1,0:T(8,128)(2,1)} %reduce-scatter.3.cloned.1.call-done, f32[2,1,3,32,3072]{4,3,2,1,0:T(8,128)} %param.18, ...), kind=kLoop, calls=%fused_computation.64 | loop fusion | flops 10616832 | bytes 9437184 | tf_op jit(solution)/shard_map/stack | solution.py:111
  240.0 1.1 pad_maximum_fusion.1
  241.2 0.0 all-gather.5.cloned.1.call-update
  241.2 0.7 copy-done.4
  241.9 9.2 %convolution_convert_fusion = bf16[1024,3072]{1,0:T(8,128)(2,1)} fusion(bf16[1024,768]{1,0:T(8,128)(2,1)S(1)} %copy-done.4, bf16[768,3072]{1,0:T(8,128)(2,1)} %bitcast.90), kind=kOutput, calls=%fused_computation.19 | convolution fusion | flops 4834983936 | bytes 12582912 | tf_op jit(solution)/shard_map/dot_general | solution.py:85
  251.1 6.6 %all-to-all-start = ((bf16[16,64,3072]{2,1,0:T(8,128)(2,1)}), bf16[16,64,3072]{2,1,0:T(8,128)(2,1)}, u32[]{:S(2)}, u32[]{:S(2)}) async-start(bf16[16,64,3072]{2,1,0:T(8,128)(2,1)} %bitcast.84), calls=%async_computation | async-start | bytes 12582912 | tf_op jit(solution)/shard_map/all_to_all | solution.py:87
  257.7 142.0 %all-to-all-done = bf16[16,64,3072]{2,1,0:T(8,128)(2,1)} async-done(((bf16[16,64,3072]{2,1,0:T(8,128)(2,1)}), bf16[16,64,3072]{2,1,0:T(8,128)(2,1)}, u32[]{:S(2)}, u32[]{:S(2)}) %all-to-all-start) | async-done | bytes 6291488 | tf_op jit(solution)/shard_map/all_to_all | solution.py:87
  399.7 4.8 %reduce_sum.12 = bf16[64,3072]{1,0:T(8,128)(2,1)} reduce(bf16[16,64,3072]{2,1,0:T(8,128)(2,1)} %all-to-all-done, bf16[]{:T(256)} %constant.78.clone.1), dimensions={0}, to_apply=%region_1.2 | reduce | flops 2949120 | bytes 6684674 | tf_op jit(solution)/shard_map/reduce_sum | solution.py:90
  404.5 4.8 %all-gather.5.cloned.1.call-done = bf16[2,24,32,3072]{3,2,1,0:T(8,128)(2,1)} async-done(((bf16[2,3,32,3072]{3,2,1,0:T(8,128)(2,1)}), bf16[2,24,32,3072]{3,2,1,0:T(8,128)(2,1)}) %all-gather.5.cloned.1.call-update) | async-done | bytes 9437200 | tf_op jit(solution)/shard_map/all_gather | solution.py:112
  409.3 9.1 %slice_bitcast_fusion.7 = (bf16[24,32,3072]{2,1,0:T(8,128)(2,1)}, bf16[24,32,3072]{2,1,0:T(8,128)(2,1)}) fusion(bf16[2,24,32,3072]{3,2,1,0:T(8,128)(2,1)} %all-gather.5.cloned.1.call-done), kind=kLoop, calls=%fused_computation.23 | loop fusion | bytes 18874368 | tf_op jit(solution)/shard_map/squeeze | solution.py:113
  418.4 5.5 %gather_fusion.10 = bf16[24,32,3072]{2,1,0:T(8,128)(2,1)} fusion(bf16[24,32,3072]{2,1,0:T(8,128)(2,1)} %get-tuple-element.12, s32[1024]{0:T(1024)S(1)} %pad_clamp_fusion.1), kind=kCustom, calls=%fused_computation.10 | custom fusion | bytes 9437280 | tf_op jit(solution)/shard_map/gather | solution.py:113
  423.9 5.5 %gather_fusion.11 = bf16[24,32,3072]{2,1,0:T(8,128)(2,1)} fusion(bf16[24,32,3072]{2,1,0:T(8,128)(2,1)} %get-tuple-element.13, s32[1024]{0:T(1024)S(1)} %pad_clamp_fusion), kind=kCustom, calls=%fused_computation.11 | custom fusion | bytes 9437280 | tf_op jit(solution)/shard_map/gather | solution.py:114
  429.4 8.4 %pad_maximum_fusion = bf16[2,768,3072]{2,1,0:T(8,128)(2,1)} fusion(bf16[1,768,3072]{2,1,0:T(8,128)(2,1)} %bitcast.83, bf16[1,768,3072]{2,1,0:T(8,128)(2,1)} %bitcast.82), kind=kLoop, calls=%fused_computation.12 | loop fusion | flops 4718592 | bytes 18874368 | tf_op jit(solution)/shard_map/stack | solution.py:115
  (24 shorter events, 0.2 us)
Async XLA Ops:
  7.2 3.9 copy-start.1
  7.2 96.2 %all-gather.3.cloned.1.call-start = ((), (), s32[]{:S(2)}) async-start(), calls=%async_computation.3 | async-start | bytes 13369344 | tf_op jit(solution)/shard_map/all_gather | solution.py:67
  9.3 167.4 %reduce-scatter.5.cloned.1.call-start = ((), (), s32[]{:S(2)}) async-start(), calls=%async_computation.5 | async-start | bytes 5308416 | tf_op jit(solution)/shard_map/reduce_scatter | solution.py:83
  35.0 77.1 %slice-start.2 = ((s8[4718592]{0:T(1024)(128)(4,1)}), s8[524288]{0:T(1024)(128)(4,1)S(1)}, s32[]{:S(2)}) async-start(s8[4718592]{0:T(1024)(128)(4,1)} %bitcast.79), calls=%async_computation.9 | async-start | bytes 1048576
  103.4 8.8 %slice-start.3 = ((s8[4718592]{0:T(1024)(128)(4,1)}), s8[4194304]{0:T(1024)(128)(4,1)S(1)}, s32[]{:S(2)}) async-start(s8[4718592]{0:T(1024)(128)(4,1)} %bitcast.79), calls=%async_computation.10 | async-start | bytes 8388608
  103.4 9.0 %copy-start = (bf16[2,1024,3072]{2,1,0:T(8,128)(2,1)S(1)}, bf16[2,1024,3072]{2,1,0:T(8,128)(2,1)}, u32[]{:S(2)}) copy-start(bf16[2,1024,3072]{2,1,0:T(8,128)(2,1)} %all-gather.3.cloned.1.call-done) | copy-start | bytes 37748740
  112.1 7.6 %copy-start.5 = (f32[1024,768]{1,0:T(8,128)}, f32[1024,768]{1,0:T(8,128)S(1)}, u32[]{:S(2)}) copy-start(f32[1024,768]{1,0:T(8,128)S(1)} %fusion.3) | copy-start | bytes 9437188
  119.8 115.6 %reduce-scatter.3.cloned.1.call-start = ((), (), s32[]{:S(2)}) async-start(), calls=%async_computation.4 | async-start | bytes 5308416 | tf_op jit(solution)/shard_map/reduce_scatter | solution.py:84
  127.2 8.2 %copy-start.2 = (s32[24]{0:T(128)S(1)}, s32[24]{0:T(128)}, u32[]{:S(2)}) copy-start(s32[24]{0:T(128)} %param.16) | copy-start | bytes 292
  127.2 21.4 %slice-start = ((s8[4718592]{0:T(1024)(128)(4,1)}), s8[524288]{0:T(1024)(128)(4,1)S(1)}, s32[]{:S(2)}) async-start(s8[4718592]{0:T(1024)(128)(4,1)} %bitcast.76), calls=%async_computation.7 | async-start | bytes 1048576
  137.7 10.9 %slice-start.1 = ((s8[4718592]{0:T(1024)(128)(4,1)}), s8[4194304]{0:T(1024)(128)(4,1)S(1)}, s32[]{:S(2)}) async-start(s8[4718592]{0:T(1024)(128)(4,1)} %bitcast.76), calls=%async_computation.8 | async-start | bytes 8388608
  148.6 10.2 %copy-start.3 = (bf16[1024,768]{1,0:T(8,128)(2,1)}, bf16[1024,768]{1,0:T(8,128)(2,1)S(1)}, u32[]{:S(2)}) copy-start(bf16[1024,768]{1,0:T(8,128)(2,1)S(1)} %fusion.10) | copy-start | bytes 4718596
  164.5 244.9 %all-gather.5.cloned.1.call-start = ((), (), s32[]{:S(2)}) async-start(), calls=%async_computation.6 | async-start | bytes 10616832 | tf_op jit(solution)/shard_map/all_gather | solution.py:112
  240.0 1.8 copy-start.4
  251.1 148.6 %all-to-all-start = ((bf16[16,64,3072]{2,1,0:T(8,128)(2,1)}), bf16[16,64,3072]{2,1,0:T(8,128)(2,1)}, u32[]{:S(2)}, u32[]{:S(2)}) async-start(bf16[16,64,3072]{2,1,0:T(8,128)(2,1)} %bitcast.84), calls=%async_computation | async-start | bytes 12582912 | tf_op jit(solution)/shard_map/all_to_all | solution.py:87
Sparse Core Ops, SparseCore 0:
  10.5 92.8 all-gather.2
  119.9 56.0 reduce-scatter.4
  178.4 56.8 reduce-scatter.2
  241.3 167.9 all-gather.4

commit v6 on v5

--- a/solution.py
+++ b/solution.py
@@ -110,9 +110,9 @@
     )
     stacked = jnp.stack([step_up, step_down])
     all_steps = lax.all_gather(stacked, "dp", axis=1, tiled=True)
-    update_up = all_steps[0][place_up].reshape(hidden_local, width)
-    update_down = all_steps[1][place_down].reshape(hidden_local, width)
-    return (input_grad, jnp.stack([update_up, update_down]))
+    places = jnp.concatenate([place_up, place_down + buckets])
+    updates = all_steps.reshape(2 * buckets, bucket_rows, width)[places]
+    return (input_grad, updates.reshape(2, hidden_local, width))
 
 
 def solution(mesh):

time: 446 us -> 427 us (0.957)
  local copies, waits for them, and re-layouts: 67.3 us -> 57.5 us
  other arithmetic: 43.8 us -> 35.5 us
    squeeze x1 -> x0, local copies, waits for them, and re-layouts: 9.1 us -> none  [layer(): update_up = all_steps[0][place_up].reshape(hidden_local, width)]
    another operation x1 -> x0, other arithmetic: 8.38 us -> none  [layer(): return (input_grad, jnp.stack([update_up, update_down]))]
    gather x2 -> x1, local copies, waits for them, and re-layouts: 11 us -> 10.2 us  [layer(): updates = all_steps.reshape(2 * buckets, bucket_rows, width)[places]]
  transfers between devices with their start and end apart: 5 -> 5, of which waited for: 4 -> 4; matrix products, arithmetic and copies ran while one was open for 23% -> 24% of each run, Pallas kernels for 0% -> 0%
where the time goes in v6:
time: 427 us; the launch traced here: 426 us
  waiting for transfers between devices  266 us (62%)
  local copies, waits for them, and re-layouts  57.5 us (13%)
  matrix products  46.3 us (11%)
  other arithmetic  35.5 us (8%)
  between operations  14 us (3%)
  starting transfers between devices  7.14 us (2%)
    all_to_all x1, waiting for transfers between devices, layer(): lax.all_to_all(partial_term.astype(jnp.bfloat16).reshape(shards_mp, local...  142 us
    all_gather x1, waiting for transfers between devices, layer(): lax.all_gather(jnp.stack([tokens_in, out_grad]), 'mp', axis=1, tiled=True)  60.2 us
    reduce_scatter x1, waiting for transfers between devices, layer(): lax.psum_scatter(up_sorted, 'dp', scatter_dimension=0, tiled=True)  58.6 us
    gather x5, local copies, waits for them, and re-layouts, owner_order(): return matrix.reshape(buckets, bucket_rows, width)[sorter]  28 us
    gather x4, local copies, waits for them, and re-layouts, owned_rows(): matrix.reshape(buckets, bucket_rows, width)[chosen].astype(jnp.float32)  11.9 us
    dot_general x1, matrix products, layer(): jnp.einsum('td,fd->tf', grad_rows, down_live, preferred_element_type=jnp....  10.8 us
    gather x1, local copies, waits for them, and re-layouts, layer(): updates = all_steps.reshape(2 * buckets, bucket_rows, width)[places]  10.2 us
    dot_general x1, matrix products, layer(): jnp.einsum('tf,td->fd', hidden_grad, feat_rows, preferred_element_type=jn...  10.2 us
  transfers between devices with their start and end apart: 5, of which 4 were waited for; matrix products, arithmetic and copies ran while one was open for 24% of the time, Pallas kernels for 0%

profile of v6, /device:TPU:0, one launch (start us, length us, event | category | flops | bytes accessed | tf_op | source)
XLA Modules:
  0.0 426.0 jit_solution(14067805888483126435)
XLA Ops:
  7.2 0.0 copy-start.1
  7.2 0.0 all-gather.3.cloned.1.call-start
  7.2 2.1 pad_maximum_fusion.1
  9.3 0.0 all-gather.3.cloned.1.call-update
  9.3 0.0 reduce-scatter.5.cloned.1.call-start
  9.4 0.7 convert_element_type.60
  10.1 0.7 convert_element_type.59
  10.8 0.1 broadcast_in_dim.40
  10.9 0.1 broadcast_in_dim.43
  11.0 0.0 copy-done.1
  11.0 1.6 sort.45
  12.7 2.7 broadcast_in_dim.45
  15.4 5.6 %gather_fusion.3 = bf16[24,32,3072]{2,1,0:T(8,128)(2,1)} fusion(bf16[24,32,3072]{2,1,0:T(8,128)(2,1)} %broadcast_in_dim.45, s32[1024]{0:T(1024)S(1)} %pad_clamp_fusion.5), kind=kCustom, calls=%fused_computation.3 | custom fusion | bytes 9437280 | tf_op jit(solution)/shard_map/gather | solution.py:56
  21.0 2.8 broadcast_in_dim.42
  23.7 5.7 %gather_fusion.1 = bf16[24,32,3072]{2,1,0:T(8,128)(2,1)} fusion(bf16[24,32,3072]{2,1,0:T(8,128)(2,1)} %broadcast_in_dim.42, s32[1024]{0:T(1024)S(1)} %pad_clamp_fusion.5), kind=kCustom, calls=%fused_computation.1 | custom fusion | bytes 9437280 | tf_op jit(solution)/shard_map/gather | solution.py:56
  29.5 5.6 %gather_fusion.2 = bf16[24,32,3072]{2,1,0:T(8,128)(2,1)} fusion(bf16[24,32,3072]{2,1,0:T(8,128)(2,1)} %bitcast.87, s32[1024]{0:T(1024)S(1)} %pad_clamp_fusion.5), kind=kCustom, calls=%fused_computation.2 | custom fusion | bytes 9437280 | tf_op jit(solution)/shard_map/gather | solution.py:56
  35.0 0.0 slice-start.2
  35.0 8.2 %mul.144 = bf16[24,32,3072]{2,1,0:T(8,128)(2,1)} multiply(bf16[24,32,3072]{2,1,0:T(8,128)(2,1)} %gather_fusion.2, bf16[24,32,3072]{2,1,0:T(8,128)(2,1)} %gather_fusion.3) | non-fusion elementwise | flops 2359296 | bytes 14155776 | tf_op jit(solution)/shard_map/mul | solution.py:63
  43.2 60.2 %all-gather.3.cloned.1.call-done = bf16[2,1024,3072]{2,1,0:T(8,128)(2,1)} async-done(((bf16[2,64,3072]{2,1,0:T(8,128)(2,1)}), bf16[2,1024,3072]{2,1,0:T(8,128)(2,1)}) %all-gather.3.cloned.1.call-update) | async-done | bytes 12582928 | tf_op jit(solution)/shard_map/all_gather | solution.py:67
  103.4 0.0 slice-start.3
  103.4 0.0 copy-start
  103.4 8.7 %fusion.3 = f32[1024,768]{1,0:T(8,128)S(1)} fusion(bf16[768,3072]{1,0:T(8,128)(2,1)} %bitcast.91, bf16[2,1024,3072]{2,1,0:T(8,128)(2,1)} %all-gather.3.cloned.1.call-done), kind=kOutput, calls=%fused_computation.19 | convolution fusion | flops 4831838208 | bytes 14155776 | tf_op jit(solution)/shard_map/td,fd->tf/dot_general | solution.py:69
  112.1 0.0 copy-start.5
  112.1 0.0 slice-done.2
  112.1 0.0 slice-done.3
  112.1 0.3 copy-done
  112.4 7.3 %fusion = bf16[768,3072]{1,0:T(8,128)(2,1)} fusion(bf16[768,3072]{1,0:T(8,128)(2,1)S(1)} %bitcast.83, bf16[2,1024,3072]{2,1,0:T(8,128)(2,1)S(1)} %copy-done, f32[1024,768]{1,0:T(8,128)S(1)} %fusion.3), kind=kOutput, calls=%fused_computation.12 | convolution fusion | flops 4845993984 | bytes 18874368 | tf_op jit(solution)/shard_map/tf,td->fd/dot_general | solution.py:73
  119.8 0.0 copy-done.5
  119.8 0.0 reduce-scatter.5.cloned.1.call-update
  119.8 0.2 reduce-scatter.3.cloned.1.call-start
  120.0 1.6 sort.47
  121.6 5.5 %gather_fusion = bf16[24,32,3072]{2,1,0:T(8,128)(2,1)} fusion(bf16[24,32,3072]{2,1,0:T(8,128)(2,1)} %bitcast.89, s32[1024]{0:T(1024)S(1)} %pad_clamp_fusion.5), kind=kCustom, calls=%fused_computation | custom fusion | bytes 9437280 | tf_op jit(solution)/shard_map/gather | solution.py:56
  127.2 8.2 %mul.142 = bf16[24,32,3072]{2,1,0:T(8,128)(2,1)} multiply(bf16[24,32,3072]{2,1,0:T(8,128)(2,1)} %gather_fusion, bf16[24,32,3072]{2,1,0:T(8,128)(2,1)} %gather_fusion.1) | non-fusion elementwise | flops 2359296 | bytes 14155776 | tf_op jit(solution)/shard_map/mul | solution.py:64
  135.3 0.0 copy-done.2
  135.4 1.6 sort.46
  137.0 0.7 gather_fusion.5
  137.7 0.0 slice-start.1
  137.7 10.8 %fusion.10 = bf16[1024,768]{1,0:T(8,128)(2,1)S(1)} fusion(f32[1024,768]{1,0:T(8,128)} %copy-done.5, bf16[768,3072]{1,0:T(8,128)(2,1)} %bitcast.93, bf16[2,1024,3072]{2,1,0:T(8,128)(2,1)} %all-gather.3.cloned.1.call-done), kind=kOutput, calls=%fused_computation.28 | convolution fusion | flops 4847566848 | bytes 15728640 | tf_op jit(solution)/shard_map/td,fd->tf/dot_general | solution.py:76
  148.6 0.0 copy-start.3
  148.6 0.0 slice-done
  148.6 0.0 slice-done.1
  148.6 10.2 %fusion.1 = bf16[768,3072]{1,0:T(8,128)(2,1)} fusion(bf16[768,3072]{1,0:T(8,128)(2,1)S(1)} %bitcast.80, bf16[1024,768]{1,0:T(8,128)(2,1)S(1)} %fusion.10, bf16[2,1024,3072]{2,1,0:T(8,128)(2,1)} %all-gather.3.cloned.1.call-done), kind=kOutput, calls=%fused_computation.14 | convolution fusion | flops 4838916096 | bytes 17301504 | tf_op jit(solution)/shard_map/tf,td->fd/dot_general | solution.py:79
  158.8 0.0 copy-done.3
  158.8 5.6 %gather_fusion.6 = bf16[24,32,3072]{2,1,0:T(8,128)(2,1)} fusion(bf16[24,32,3072]{2,1,0:T(8,128)(2,1)} %bitcast.95, s32[1024]{0:T(1024)S(1)} %pad_clamp_fusion.2), kind=kCustom, calls=%fused_computation.6 | custom fusion | bytes 9437280 | tf_op jit(solution)/shard_map/gather | solution.py:56
  164.4 0.0 reduce-scatter.3.cloned.1.call-update
  164.4 0.3 all-gather.5.cloned.1.call-start
  164.7 0.1 compare_select_fusion.1
  164.8 3.0 gather_fusion.7
  167.8 3.0 gather_fusion.4
  170.8 3.0 gather_fusion.9
  173.8 3.0 gather_fusion.8
  176.7 0.0 reduce-scatter.5.cloned.1.call-done
  176.8 58.6 %reduce-scatter.3.cloned.1.call-done = bf16[3,32,3072]{2,1,0:T(8,128)(2,1)} async-done(((bf16[24,32,3072]{2,1,0:T(8,128)(2,1)}), bf16[3,32,3072]{2,1,0:T(8,128)(2,1)}) %reduce-scatter.3.cloned.1.call-update) | async-done | bytes 589840 | tf_op jit(solution)/shard_map/reduce_scatter | solution.py:84
  235.4 4.7 %fusion.35 = (bf16[1,3,32,3072]{3,2,1,0:T(8,128)(2,1)S(1)}, bf16[1,3,32,3072]{3,2,1,0:T(8,128)(2,1)S(1)}) fusion(bf16[3,32,3072]{2,1,0:T(8,128)(2,1)S(1)} %gather_fusion.7, f32[2,1,3,32,3072]{4,3,2,1,0:T(8,128)} %param.19, bf16[3,32,3072]{2,1,0:T(8,128)(2,1)} %reduce-scatter.3.cloned.1.call-done, f32[2,1,3,32,3072]{4,3,2,1,0:T(8,128)} %param.18, ...), kind=kLoop, calls=%fused_computation.60 | loop fusion | flops 10616832 | bytes 9437184 | tf_op jit(solution)/shard_map/stack | solution.py:111
  240.0 1.1 pad_maximum_fusion
  241.2 0.0 all-gather.5.cloned.1.call-update
  241.2 0.7 copy-done.4
  241.9 9.2 %convolution_convert_fusion = bf16[1024,3072]{1,0:T(8,128)(2,1)} fusion(bf16[1024,768]{1,0:T(8,128)(2,1)S(1)} %copy-done.4, bf16[768,3072]{1,0:T(8,128)(2,1)} %bitcast.92), kind=kOutput, calls=%fused_computation.17 | convolution fusion | flops 4834983936 | bytes 12582912 | tf_op jit(solution)/shard_map/dot_general | solution.py:85
  251.1 6.6 %all-to-all-start = ((bf16[16,64,3072]{2,1,0:T(8,128)(2,1)}), bf16[16,64,3072]{2,1,0:T(8,128)(2,1)}, u32[]{:S(2)}, u32[]{:S(2)}) async-start(bf16[16,64,3072]{2,1,0:T(8,128)(2,1)} %bitcast.86), calls=%async_computation | async-start | bytes 12582912 | tf_op jit(solution)/shard_map/all_to_all | solution.py:87
  257.7 0.1 fusion.42
  257.8 141.9 %all-to-all-done = bf16[16,64,3072]{2,1,0:T(8,128)(2,1)} async-done(((bf16[16,64,3072]{2,1,0:T(8,128)(2,1)}), bf16[16,64,3072]{2,1,0:T(8,128)(2,1)}, u32[]{:S(2)}, u32[]{:S(2)}) %all-to-all-start) | async-done | bytes 6291488 | tf_op jit(solution)/shard_map/all_to_all | solution.py:87
  399.7 4.8 %reduce_sum.12 = bf16[64,3072]{1,0:T(8,128)(2,1)} reduce(bf16[16,64,3072]{2,1,0:T(8,128)(2,1)} %all-to-all-done, bf16[]{:T(256)} %constant.80.clone.1), dimensions={0}, to_apply=%region_1.2 | reduce | flops 2949120 | bytes 6684674 | tf_op jit(solution)/shard_map/reduce_sum | solution.py:90
  404.5 4.8 %all-gather.5.cloned.1.call-done = bf16[2,24,32,3072]{3,2,1,0:T(8,128)(2,1)} async-done(((bf16[2,3,32,3072]{3,2,1,0:T(8,128)(2,1)}), bf16[2,24,32,3072]{3,2,1,0:T(8,128)(2,1)}) %all-gather.5.cloned.1.call-update) | async-done | bytes 9437200 | tf_op jit(solution)/shard_map/all_gather | solution.py:112
  409.3 10.2 %gather_fusion.10 = bf16[48,32,3072]{2,1,0:T(8,128)(2,1)} fusion(bf16[48,32,3072]{2,1,0:T(8,128)(2,1)} %bitcast.84, s32[1024]{0:T(1024)S(1)} %pad_clamp_fusion), kind=kCustom, calls=%fused_computation.10 | custom fusion | bytes 18874560 | tf_op jit(solution)/shard_map/gather | solution.py:114
  (22 shorter events, 0.2 us)
Async XLA Ops:
  7.2 3.8 copy-start.1
  7.2 96.2 %all-gather.3.cloned.1.call-start = ((), (), s32[]{:S(2)}) async-start(), calls=%async_computation.3 | async-start | bytes 13369344 | tf_op jit(solution)/shard_map/all_gather | solution.py:67
  9.3 167.5 %reduce-scatter.5.cloned.1.call-start = ((), (), s32[]{:S(2)}) async-start(), calls=%async_computation.5 | async-start | bytes 5308416 | tf_op jit(solution)/shard_map/reduce_scatter | solution.py:83
  35.0 77.1 %slice-start.2 = ((s8[4718592]{0:T(1024)(128)(4,1)}), s8[524288]{0:T(1024)(128)(4,1)S(1)}, s32[]{:S(2)}) async-start(s8[4718592]{0:T(1024)(128)(4,1)} %bitcast.81), calls=%async_computation.9 | async-start | bytes 1048576
  103.4 8.8 %slice-start.3 = ((s8[4718592]{0:T(1024)(128)(4,1)}), s8[4194304]{0:T(1024)(128)(4,1)S(1)}, s32[]{:S(2)}) async-start(s8[4718592]{0:T(1024)(128)(4,1)} %bitcast.81), calls=%async_computation.10 | async-start | bytes 8388608
  103.4 9.0 %copy-start = (bf16[2,1024,3072]{2,1,0:T(8,128)(2,1)S(1)}, bf16[2,1024,3072]{2,1,0:T(8,128)(2,1)}, u32[]{:S(2)}) copy-start(bf16[2,1024,3072]{2,1,0:T(8,128)(2,1)} %all-gather.3.cloned.1.call-done) | copy-start | bytes 37748740
  112.1 7.6 %copy-start.5 = (f32[1024,768]{1,0:T(8,128)}, f32[1024,768]{1,0:T(8,128)S(1)}, u32[]{:S(2)}) copy-start(f32[1024,768]{1,0:T(8,128)S(1)} %fusion.3) | copy-start | bytes 9437188
  119.8 115.6 %reduce-scatter.3.cloned.1.call-start = ((), (), s32[]{:S(2)}) async-start(), calls=%async_computation.4 | async-start | bytes 5308416 | tf_op jit(solution)/shard_map/reduce_scatter | solution.py:84
  127.2 8.2 %copy-start.2 = (s32[24]{0:T(128)S(1)}, s32[24]{0:T(128)}, u32[]{:S(2)}) copy-start(s32[24]{0:T(128)} %param.16) | copy-start | bytes 292
  127.2 21.4 %slice-start = ((s8[4718592]{0:T(1024)(128)(4,1)}), s8[524288]{0:T(1024)(128)(4,1)S(1)}, s32[]{:S(2)}) async-start(s8[4718592]{0:T(1024)(128)(4,1)} %bitcast.78), calls=%async_computation.7 | async-start | bytes 1048576
  137.7 10.9 %slice-start.1 = ((s8[4718592]{0:T(1024)(128)(4,1)}), s8[4194304]{0:T(1024)(128)(4,1)S(1)}, s32[]{:S(2)}) async-start(s8[4718592]{0:T(1024)(128)(4,1)} %bitcast.78), calls=%async_computation.8 | async-start | bytes 8388608
  148.6 10.2 %copy-start.3 = (bf16[1024,768]{1,0:T(8,128)(2,1)}, bf16[1024,768]{1,0:T(8,128)(2,1)S(1)}, u32[]{:S(2)}) copy-start(bf16[1024,768]{1,0:T(8,128)(2,1)S(1)} %fusion.10) | copy-start | bytes 4718596
  164.4 244.9 %all-gather.5.cloned.1.call-start = ((), (), s32[]{:S(2)}) async-start(), calls=%async_computation.6 | async-start | bytes 10616832 | tf_op jit(solution)/shard_map/all_gather | solution.py:112
  240.0 1.8 copy-start.4
  251.1 148.6 %all-to-all-start = ((bf16[16,64,3072]{2,1,0:T(8,128)(2,1)}), bf16[16,64,3072]{2,1,0:T(8,128)(2,1)}, u32[]{:S(2)}, u32[]{:S(2)}) async-start(bf16[16,64,3072]{2,1,0:T(8,128)(2,1)} %bitcast.86), calls=%async_computation | async-start | bytes 12582912 | tf_op jit(solution)/shard_map/all_to_all | solution.py:87
Sparse Core Ops, SparseCore 0:
  10.5 92.8 all-gather.2
  119.9 56.0 reduce-scatter.4
  178.4 56.8 reduce-scatter.2
  241.3 167.9 all-gather.4

commit v7 on v6

--- a/solution.py
+++ b/solution.py
@@ -110,8 +110,14 @@
     )
     stacked = jnp.stack([step_up, step_down])
     all_steps = lax.all_gather(stacked, "dp", axis=1, tiled=True)
-    places = jnp.concatenate([place_up, place_down + buckets])
-    updates = all_steps.reshape(2 * buckets, bucket_rows, width)[places]
+    places = jnp.stack([place_up, place_down])
+    chooser = (places[:, :, None] == jnp.arange(buckets)[None, None, :]).astype(jnp.bfloat16)
+    updates = jnp.einsum(
+        "sbk,skx->sbx",
+        chooser,
+        all_steps.reshape(2, buckets, bucket_rows * width),
+        preferred_element_type=jnp.float32,
+    ).astype(jnp.bfloat16)
     return (input_grad, updates.reshape(2, hidden_local, width))
 
 

time: 427 us -> 448 us (1.049)
  local copies, waits for them, and re-layouts: 57.5 us -> 68.3 us
  matrix products: 46.3 us -> 56.5 us
    reshape x0 -> x2, local copies, waits for them, and re-layouts: none -> 21 us  [the longest x1 10.5 us: layer(): return (input_grad, updates.reshape(2, hidden_local, width))]
    gather x1 -> x0, local copies, waits for them, and re-layouts: 10.2 us -> none  [layer(): updates = all_steps.reshape(2 * buckets, bucket_rows, width)[places]]
    dot_general x0 -> x1, matrix products: none -> 9.96 us  [layer(): jnp.einsum('sbk,skx->sbx', chooser, all_steps.reshape(2, buckets, bucket_...]
  transfers between devices with their start and end apart: 5 -> 5, of which waited for: 4 -> 4; matrix products, arithmetic and copies ran while one was open for 24% -> 23% of each run, Pallas kernels for 0% -> 0%
where the time goes in v7:
time: 448 us; the launch traced here: 447 us
  waiting for transfers between devices  265 us (59%)
  local copies, waits for them, and re-layouts  68.3 us (15%)
  matrix products  56.5 us (13%)
  other arithmetic  35.4 us (8%)
  between operations  14 us (3%)
  starting transfers between devices  7.13 us (2%)
    all_to_all x1, waiting for transfers between devices, layer(): lax.all_to_all(partial_term.astype(jnp.bfloat16).reshape(shards_mp, local...  142 us
    all_gather x1, waiting for transfers between devices, layer(): lax.all_gather(jnp.stack([tokens_in, out_grad]), 'mp', axis=1, tiled=True)  60.2 us
    reduce_scatter x1, waiting for transfers between devices, layer(): lax.psum_scatter(up_sorted, 'dp', scatter_dimension=0, tiled=True)  58.4 us
    gather x5, local copies, waits for them, and re-layouts, owner_order(): return matrix.reshape(buckets, bucket_rows, width)[sorter]  28 us
    gather x4, local copies, waits for them, and re-layouts, owned_rows(): matrix.reshape(buckets, bucket_rows, width)[chosen].astype(jnp.float32)  11.9 us
    dot_general x1, matrix products, layer(): jnp.einsum('td,fd->tf', grad_rows, down_live, preferred_element_type=jnp....  10.9 us
    reshape x1, local copies, waits for them, and re-layouts, layer(): return (input_grad, updates.reshape(2, hidden_local, width))  10.5 us
    reshape x1, local copies, waits for them, and re-layouts, layer(): all_steps.reshape(2, buckets, bucket_rows * width)  10.5 us
  transfers between devices with their start and end apart: 5, of which 4 were waited for; matrix products, arithmetic and copies ran while one was open for 23% of the time, Pallas kernels for 0%

profile of v7, /device:TPU:0, one launch (start us, length us, event | category | flops | bytes accessed | tf_op | source)
XLA Modules:
  0.0 446.8 jit_solution(8124630633058552110)
XLA Ops:
  7.2 0.0 copy-start.2
  7.2 0.0 all-gather.3.cloned.1.call-start
  7.2 2.1 pad_maximum_fusion.1
  9.3 0.0 all-gather.3.cloned.1.call-update
  9.3 0.0 reduce-scatter.5.cloned.1.call-start
  9.4 0.7 convert_element_type.64
  10.1 0.7 convert_element_type.63
  10.8 0.1 broadcast_in_dim.41
  10.9 0.1 broadcast_in_dim.44
  11.0 0.0 copy-done.2
  11.0 1.6 sort.45
  12.7 2.7 broadcast_in_dim.46
  15.4 5.6 %gather_fusion.3 = bf16[24,32,3072]{2,1,0:T(8,128)(2,1)} fusion(bf16[24,32,3072]{2,1,0:T(8,128)(2,1)} %broadcast_in_dim.46, s32[1024]{0:T(1024)S(1)} %pad_clamp_fusion.4), kind=kCustom, calls=%fused_computation.3 | custom fusion | bytes 9437280 | tf_op jit(solution)/shard_map/gather | solution.py:56
  21.0 2.8 broadcast_in_dim.43
  23.7 5.7 %gather_fusion.1 = bf16[24,32,3072]{2,1,0:T(8,128)(2,1)} fusion(bf16[24,32,3072]{2,1,0:T(8,128)(2,1)} %broadcast_in_dim.43, s32[1024]{0:T(1024)S(1)} %pad_clamp_fusion.4), kind=kCustom, calls=%fused_computation.1 | custom fusion | bytes 9437280 | tf_op jit(solution)/shard_map/gather | solution.py:56
  29.5 5.6 %gather_fusion.2 = bf16[24,32,3072]{2,1,0:T(8,128)(2,1)} fusion(bf16[24,32,3072]{2,1,0:T(8,128)(2,1)} %bitcast.84, s32[1024]{0:T(1024)S(1)} %pad_clamp_fusion.4), kind=kCustom, calls=%fused_computation.2 | custom fusion | bytes 9437280 | tf_op jit(solution)/shard_map/gather | solution.py:56
  35.0 0.0 slice-start.2
  35.0 8.2 %mul.144 = bf16[24,32,3072]{2,1,0:T(8,128)(2,1)} multiply(bf16[24,32,3072]{2,1,0:T(8,128)(2,1)} %gather_fusion.2, bf16[24,32,3072]{2,1,0:T(8,128)(2,1)} %gather_fusion.3) | non-fusion elementwise | flops 2359296 | bytes 14155776 | tf_op jit(solution)/shard_map/mul | solution.py:63
  43.2 60.2 %all-gather.3.cloned.1.call-done = bf16[2,1024,3072]{2,1,0:T(8,128)(2,1)} async-done(((bf16[2,64,3072]{2,1,0:T(8,128)(2,1)}), bf16[2,1024,3072]{2,1,0:T(8,128)(2,1)}) %all-gather.3.cloned.1.call-update) | async-done | bytes 12582928 | tf_op jit(solution)/shard_map/all_gather | solution.py:67
  103.4 0.0 slice-start.3
  103.4 8.7 %fusion.3 = f32[1024,768]{1,0:T(8,128)S(1)} fusion(bf16[768,3072]{1,0:T(8,128)(2,1)} %bitcast.88, bf16[2,1024,3072]{2,1,0:T(8,128)(2,1)} %all-gather.3.cloned.1.call-done), kind=kOutput, calls=%fused_computation.19 | convolution fusion | flops 4831838208 | bytes 14155776 | tf_op jit(solution)/shard_map/td,fd->tf/dot_general | solution.py:69
  112.1 0.0 copy-start.5
  112.1 0.0 slice-done.2
  112.1 0.0 slice-done.3
  112.2 0.3 copy-done
  112.4 7.3 %fusion = bf16[768,3072]{1,0:T(8,128)(2,1)} fusion(bf16[768,3072]{1,0:T(8,128)(2,1)S(1)} %bitcast.82, bf16[2,1024,3072]{2,1,0:T(8,128)(2,1)S(1)} %copy-done, f32[1024,768]{1,0:T(8,128)S(1)} %fusion.3), kind=kOutput, calls=%fused_computation.12 | convolution fusion | flops 4845993984 | bytes 18874368 | tf_op jit(solution)/shard_map/tf,td->fd/dot_general | solution.py:73
  119.8 0.0 copy-done.5
  119.8 0.0 reduce-scatter.5.cloned.1.call-update
  119.8 0.2 reduce-scatter.3.cloned.1.call-start
  120.0 1.6 sort.47
  121.6 5.5 %gather_fusion = bf16[24,32,3072]{2,1,0:T(8,128)(2,1)} fusion(bf16[24,32,3072]{2,1,0:T(8,128)(2,1)} %bitcast.86, s32[1024]{0:T(1024)S(1)} %pad_clamp_fusion.4), kind=kCustom, calls=%fused_computation | custom fusion | bytes 9437280 | tf_op jit(solution)/shard_map/gather | solution.py:56
  127.2 8.2 %mul.142 = bf16[24,32,3072]{2,1,0:T(8,128)(2,1)} multiply(bf16[24,32,3072]{2,1,0:T(8,128)(2,1)} %gather_fusion, bf16[24,32,3072]{2,1,0:T(8,128)(2,1)} %gather_fusion.1) | non-fusion elementwise | flops 2359296 | bytes 14155776 | tf_op jit(solution)/shard_map/mul | solution.py:64
  135.3 0.0 copy-done.1
  135.4 1.6 sort.46
  137.0 0.7 gather_fusion.5
  137.7 0.0 slice-start.1
  137.7 10.9 %fusion.10 = bf16[1024,768]{1,0:T(8,128)(2,1)S(1)} fusion(f32[1024,768]{1,0:T(8,128)} %copy-done.5, bf16[768,3072]{1,0:T(8,128)(2,1)} %bitcast.90, bf16[2,1024,3072]{2,1,0:T(8,128)(2,1)} %all-gather.3.cloned.1.call-done), kind=kOutput, calls=%fused_computation.28 | convolution fusion | flops 4847566848 | bytes 15728640 | tf_op jit(solution)/shard_map/td,fd->tf/dot_general | solution.py:76
  148.6 0.0 copy-start.3
  148.6 0.0 slice-done
  148.6 0.0 slice-done.1
  148.6 10.3 %fusion.1 = bf16[768,3072]{1,0:T(8,128)(2,1)} fusion(bf16[768,3072]{1,0:T(8,128)(2,1)S(1)} %bitcast.79, bf16[1024,768]{1,0:T(8,128)(2,1)S(1)} %fusion.10, bf16[2,1024,3072]{2,1,0:T(8,128)(2,1)} %all-gather.3.cloned.1.call-done), kind=kOutput, calls=%fused_computation.14 | convolution fusion | flops 4838916096 | bytes 17301504 | tf_op jit(solution)/shard_map/tf,td->fd/dot_general | solution.py:79
  159.0 0.0 copy-done.3
  159.0 5.6 %gather_fusion.6 = bf16[24,32,3072]{2,1,0:T(8,128)(2,1)} fusion(bf16[24,32,3072]{2,1,0:T(8,128)(2,1)} %bitcast.92, s32[1024]{0:T(1024)S(1)} %pad_clamp_fusion.1), kind=kCustom, calls=%fused_computation.6 | custom fusion | bytes 9437280 | tf_op jit(solution)/shard_map/gather | solution.py:56
  164.6 0.0 reduce-scatter.3.cloned.1.call-update
  164.6 0.3 all-gather.5.cloned.1.call-start
  164.9 0.1 compare_select_fusion
  165.0 3.0 gather_fusion.7
  167.9 3.0 gather_fusion.4
  170.9 3.0 gather_fusion.9
  173.9 3.0 gather_fusion.8
  176.9 0.0 reduce-scatter.5.cloned.1.call-done
  176.9 58.4 %reduce-scatter.3.cloned.1.call-done = bf16[3,32,3072]{2,1,0:T(8,128)(2,1)} async-done(((bf16[24,32,3072]{2,1,0:T(8,128)(2,1)}), bf16[3,32,3072]{2,1,0:T(8,128)(2,1)}) %reduce-scatter.3.cloned.1.call-update) | async-done | bytes 589840 | tf_op jit(solution)/shard_map/reduce_scatter | solution.py:84
  235.4 4.7 %fusion.35 = (bf16[1,3,32,3072]{3,2,1,0:T(8,128)(2,1)S(1)}, bf16[1,3,32,3072]{3,2,1,0:T(8,128)(2,1)S(1)}) fusion(bf16[3,32,3072]{2,1,0:T(8,128)(2,1)S(1)} %gather_fusion.7, f32[2,1,3,32,3072]{4,3,2,1,0:T(8,128)} %param.19, bf16[3,32,3072]{2,1,0:T(8,128)(2,1)} %reduce-scatter.3.cloned.1.call-done, f32[2,1,3,32,3072]{4,3,2,1,0:T(8,128)} %param.18, ...), kind=kLoop, calls=%fused_computation.60 | loop fusion | flops 10616832 | bytes 9437184 | tf_op jit(solution)/shard_map/stack | solution.py:111
  240.0 1.1 pad_maximum_fusion
  241.2 0.0 all-gather.5.cloned.1.call-update
  241.2 0.7 copy-done.4
  241.9 9.2 %convolution_convert_fusion.1 = bf16[1024,3072]{1,0:T(8,128)(2,1)} fusion(bf16[1024,768]{1,0:T(8,128)(2,1)S(1)} %copy-done.4, bf16[768,3072]{1,0:T(8,128)(2,1)} %bitcast.89), kind=kOutput, calls=%fused_computation.17 | convolution fusion | flops 4834983936 | bytes 12582912 | tf_op jit(solution)/shard_map/dot_general | solution.py:85
  251.1 6.6 %all-to-all-start = ((bf16[16,64,3072]{2,1,0:T(8,128)(2,1)}), bf16[16,64,3072]{2,1,0:T(8,128)(2,1)}, u32[]{:S(2)}, u32[]{:S(2)}) async-start(bf16[16,64,3072]{2,1,0:T(8,128)(2,1)} %bitcast.83), calls=%async_computation | async-start | bytes 12582912 | tf_op jit(solution)/shard_map/all_to_all | solution.py:87
  257.7 142.0 %all-to-all-done = bf16[16,64,3072]{2,1,0:T(8,128)(2,1)} async-done(((bf16[16,64,3072]{2,1,0:T(8,128)(2,1)}), bf16[16,64,3072]{2,1,0:T(8,128)(2,1)}, u32[]{:S(2)}, u32[]{:S(2)}) %all-to-all-start) | async-done | bytes 6291488 | tf_op jit(solution)/shard_map/all_to_all | solution.py:87
  399.7 4.8 %reduce_sum.12 = bf16[64,3072]{1,0:T(8,128)(2,1)} reduce(bf16[16,64,3072]{2,1,0:T(8,128)(2,1)} %all-to-all-done, bf16[]{:T(256)} %constant.78.clone.1), dimensions={0}, to_apply=%region_1.2 | reduce | flops 2949120 | bytes 6684674 | tf_op jit(solution)/shard_map/reduce_sum | solution.py:90
  404.5 4.8 %all-gather.5.cloned.1.call-done = bf16[2,24,32,3072]{3,2,1,0:T(8,128)(2,1)} async-done(((bf16[2,3,32,3072]{3,2,1,0:T(8,128)(2,1)}), bf16[2,24,32,3072]{3,2,1,0:T(8,128)(2,1)}) %all-gather.5.cloned.1.call-update) | async-done | bytes 9437200 | tf_op jit(solution)/shard_map/all_gather | solution.py:112
  409.3 10.5 %reshape.87 = bf16[2,24,98304]{2,1,0:T(8,128)(2,1)} reshape(bf16[2,24,32,3072]{3,2,1,0:T(8,128)(2,1)} %all-gather.5.cloned.1.call-done) | data formatting | bytes 18874368 | tf_op jit(solution)/shard_map/reshape | solution.py:118
  419.8 10.0 %convolution_convert_fusion = bf16[2,24,98304]{2,1,0:T(8,128)(2,1)} fusion(bf16[2,24,98304]{2,1,0:T(8,128)(2,1)} %reshape.87, s32[2,24]{1,0:T(2,128)S(1)} %pad_add_fusion), kind=kOutput, calls=%fused_computation.10 | convolution fusion | flops 231212160 | bytes 18874560 | tf_op jit(solution)/shard_map/sbk,skx->sbx/dot_general | solution.py:115
  429.8 10.5 %reshape.88 = bf16[2,768,3072]{2,1,0:T(8,128)(2,1)} reshape(bf16[2,24,98304]{2,1,0:T(8,128)(2,1)} %convolution_convert_fusion) | data formatting | bytes 18874368 | tf_op jit(solution)/shard_map/reshape | solution.py:121
  (24 shorter events, 0.2 us)
Async XLA Ops:
  7.2 3.8 copy-start.2
  7.2 96.2 %all-gather.3.cloned.1.call-start = ((), (), s32[]{:S(2)}) async-start(), calls=%async_computation.3 | async-start | bytes 13369344 | tf_op jit(solution)/shard_map/all_gather | solution.py:67
  9.3 167.6 %reduce-scatter.5.cloned.1.call-start = ((), (), s32[]{:S(2)}) async-start(), calls=%async_computation.5 | async-start | bytes 5308416 | tf_op jit(solution)/shard_map/reduce_scatter | solution.py:83
  35.0 77.1 %slice-start.2 = ((s8[4718592]{0:T(1024)(128)(4,1)}), s8[524288]{0:T(1024)(128)(4,1)S(1)}, s32[]{:S(2)}) async-start(s8[4718592]{0:T(1024)(128)(4,1)} %bitcast.80), calls=%async_computation.9 | async-start | bytes 1048576
  103.4 8.8 %slice-start.3 = ((s8[4718592]{0:T(1024)(128)(4,1)}), s8[4194304]{0:T(1024)(128)(4,1)S(1)}, s32[]{:S(2)}) async-start(s8[4718592]{0:T(1024)(128)(4,1)} %bitcast.80), calls=%async_computation.10 | async-start | bytes 8388608
  103.4 9.0 %copy-start = (bf16[2,1024,3072]{2,1,0:T(8,128)(2,1)S(1)}, bf16[2,1024,3072]{2,1,0:T(8,128)(2,1)}, u32[]{:S(2)}) copy-start(bf16[2,1024,3072]{2,1,0:T(8,128)(2,1)} %all-gather.3.cloned.1.call-done) | copy-start | bytes 37748740
  112.1 7.6 %copy-start.5 = (f32[1024,768]{1,0:T(8,128)}, f32[1024,768]{1,0:T(8,128)S(1)}, u32[]{:S(2)}) copy-start(f32[1024,768]{1,0:T(8,128)S(1)} %fusion.3) | copy-start | bytes 9437188
  119.8 115.6 %reduce-scatter.3.cloned.1.call-start = ((), (), s32[]{:S(2)}) async-start(), calls=%async_computation.4 | async-start | bytes 5308416 | tf_op jit(solution)/shard_map/reduce_scatter | solution.py:84
  127.2 8.2 %copy-start.1 = (s32[24]{0:T(128)S(1)}, s32[24]{0:T(128)}, u32[]{:S(2)}) copy-start(s32[24]{0:T(128)} %param.16) | copy-start | bytes 292
  127.2 21.4 %slice-start = ((s8[4718592]{0:T(1024)(128)(4,1)}), s8[524288]{0:T(1024)(128)(4,1)S(1)}, s32[]{:S(2)}) async-start(s8[4718592]{0:T(1024)(128)(4,1)} %bitcast.77), calls=%async_computation.7 | async-start | bytes 1048576
  137.7 10.9 %slice-start.1 = ((s8[4718592]{0:T(1024)(128)(4,1)}), s8[4194304]{0:T(1024)(128)(4,1)S(1)}, s32[]{:S(2)}) async-start(s8[4718592]{0:T(1024)(128)(4,1)} %bitcast.77), calls=%async_computation.8 | async-start | bytes 8388608
  148.6 10.4 %copy-start.3 = (bf16[1024,768]{1,0:T(8,128)(2,1)}, bf16[1024,768]{1,0:T(8,128)(2,1)S(1)}, u32[]{:S(2)}) copy-start(bf16[1024,768]{1,0:T(8,128)(2,1)S(1)} %fusion.10) | copy-start | bytes 4718596
  164.6 244.7 %all-gather.5.cloned.1.call-start = ((), (), s32[]{:S(2)}) async-start(), calls=%async_computation.6 | async-start | bytes 10616832 | tf_op jit(solution)/shard_map/all_gather | solution.py:112
  240.0 1.8 copy-start.4
  251.1 148.6 %all-to-all-start = ((bf16[16,64,3072]{2,1,0:T(8,128)(2,1)}), bf16[16,64,3072]{2,1,0:T(8,128)(2,1)}, u32[]{:S(2)}, u32[]{:S(2)}) async-start(bf16[16,64,3072]{2,1,0:T(8,128)(2,1)} %bitcast.83), calls=%async_computation | async-start | bytes 12582912 | tf_op jit(solution)/shard_map/all_to_all | solution.py:87
Sparse Core Ops, SparseCore 0:
  10.5 92.8 all-gather.2
  119.9 56.0 reduce-scatter.4
  178.4 56.8 reduce-scatter.2
  241.3 167.9 all-gather.4
